TPU v7x, 32 devices: a whole 2x2x4 slice. The times are simulated.
32 devices in a mesh: tile: 8 (over z, x), chan: 4 (over y, core).
Axes of the slice: x: 2, y: 2, z: 4, core: 2. Of those that a mesh axis runs over, the one named last changes fastest.
Arguments:
- visibilities: float32 [4, 2048, 128], P('chan', 'tile'), may hold values from -6 to 6
- kernels: bfloat16 [4, 32, 2, 64, 128], P('chan'), may hold values from -0.75 to 0.75
- destination: int32 [4, 2048, 1], P('chan', 'tile'), may hold values from 0 to 7; in each aligned block of 256 rows (0 to 255, 256 to 511, ..., all dimensions but the last counted through in order) at most 96 rows name the same one
- cell: int32 [4, 2048], P('chan', 'tile'), may hold values from 0 to 2047
- plane: int32 [4, 2048], P('chan', 'tile'), may hold values from 0 to 31
Outputs:
- image: float32 [1024, 1024], P('chan', 'tile')
Inputs may be any that keep to these rules, and one draw needn't show every extreme that they name: `destination`: in the rows of one device (aligned blocks of 256 rows), no tile is named more than 96 times; some tile is named exactly 96 times in some devices' rows.
All inputs are finite; a program needn't handle non-finite values.
Results may differ from a plain program's by a relative error of at most 0.0059.
Values may be sent and summed in bfloat16 or wider, within the bound.
No kernel may reach another device: no remote copies, remote signals or barrier semaphores. Data moves between devices by JAX's collectives and lax.ppermute only.
A program may use at most 384 MiB of HBM per device.

v0:
```python
import math

import jax
import jax.numpy as jnp
from jax import lax
from jax.sharding import PartitionSpec as P

G = 8192
S = 64
NW = 32
P_SIZE = 1024
NF = 8


def block_patches(samples, kernel_rows):
    sample_count = samples.shape[1] // 2
    support = kernel_rows.shape[3] // 2
    vis_real = samples[:, :sample_count, None]
    vis_imag = samples[:, sample_count:, None]
    kern_real = kernel_rows[:, 0].astype(jnp.float32)
    kern_imag = kernel_rows[:, 1].astype(jnp.float32)
    full_real = (vis_real * kern_real - vis_imag * kern_imag).astype(jnp.bfloat16)
    full_imag = (vis_real * kern_imag + vis_imag * kern_real).astype(jnp.bfloat16)
    weighted_real = full_real[:, :, support:]
    weighted_imag = full_imag[:, :, support:]
    v_weighted = jnp.stack(
        [
            jnp.concatenate([weighted_real, weighted_imag], axis=-1),
            jnp.concatenate([-weighted_imag, weighted_real], axis=-1),
        ],
        1,
    )
    patch = jnp.einsum("bpkx,bpkn->bxn", kernel_rows, v_weighted, preferred_element_type=jnp.float32)
    return patch[:, :support, :]


def phase_index(rows, cols):
    spacing = G // P_SIZE - 1
    return jnp.mod(rows[:, None] * (spacing * cols[None, :]), G)


def cos_sin_f32(index):
    angle = index.astype(jnp.float32) * (2.0 * math.pi / G)
    return jnp.cos(angle), jnp.sin(angle)


def local(visibilities, kernels, destination, cell, plane):
    tile_count = lax.axis_size("tile")
    tile_index = lax.axis_index("tile")
    samples = visibilities[0]
    kernel_set = kernels[0]
    owners = destination[0, :, 0]
    blocks = samples.shape[0]
    capacity = 3 * blocks // tile_count
    spacing = G // P_SIZE - 1

    counts = jnp.sum(
        (owners[:, None] == jnp.arange(tile_count, dtype=jnp.int32)[None, :]).astype(jnp.int32), axis=0
    )
    first = jnp.cumsum(counts) - counts
    order = jnp.argsort(owners, stable=True).astype(jnp.int32)
    slot = jnp.arange(capacity, dtype=jnp.int32)
    valid = slot[None, :] < counts[:, None]
    src = order[jnp.clip(first[:, None] + slot[None, :], 0, blocks - 1)]
    packed_meta = cell[0] * NW + plane[0]
    send_samples = jnp.where(valid[:, :, None], samples[src], 0.0)
    send_meta = jnp.where(valid, packed_meta[src], 0)
    arrived = lax.all_to_all(send_samples, "tile", split_axis=0, concat_axis=0, tiled=True)
    arrived_meta = lax.all_to_all(send_meta, "tile", split_axis=0, concat_axis=0, tiled=True)
    slot_total = tile_count * capacity
    arrived = arrived.reshape(slot_total, samples.shape[1])
    arrived_meta = arrived_meta.reshape(slot_total)

    slab_rows = G // tile_count
    row_cells = slab_rows // S
    cell_cols = G // S
    q_len = G // NF
    q_cells = q_len // S
    j_len = P_SIZE // NF

    cell_r = arrived_meta // NW
    plane_r = arrived_meta % NW
    patches = block_patches(arrived, kernel_set[plane_r])
    rotated = jnp.concatenate([-patches[:, :, S:], patches[:, :, :S]], axis=-1)
    p2 = jnp.stack([patches, rotated], axis=1).astype(jnp.bfloat16).reshape(slot_total, 2, S * 2 * S)

    a_s = cell_r // cell_cols
    cc_s = cell_r % cell_cols
    p_s = cc_s // q_cells
    qc_s = cc_s % q_cells
    resid = jnp.arange(NF, dtype=jnp.int32)
    ph_index = jnp.mod(spacing * (p_s[:, None] - NF // 2) * resid[None, :], NF)
    ph_angle = ph_index.astype(jnp.float32) * (2.0 * math.pi / NF)
    phase = jnp.stack([jnp.cos(ph_angle), jnp.sin(ph_angle)], axis=-1)
    place = (a_s[:, None] == jnp.arange(row_cells, dtype=jnp.int32)[None, :])[:, :, None] & (
        qc_s[:, None] == jnp.arange(q_cells, dtype=jnp.int32)[None, :]
    )[:, None, :]
    l2 = (place.astype(jnp.float32)[None, :, :, :, None] * jnp.transpose(phase, (1, 0, 2))[:, :, None, None, :])
    l2 = jnp.transpose(l2, (0, 2, 3, 1, 4)).astype(jnp.bfloat16)
    folded = jnp.einsum("raqsk,skn->raqn", l2, p2, preferred_element_type=jnp.float32).astype(jnp.bfloat16)
    folded = folded.reshape(NF, row_cells, q_cells, S, 2 * S)

    j_index = resid[:, None] + NF * (jnp.arange(j_len, dtype=jnp.int32)[None, :] - j_len // 2)
    coarse = jnp.arange(q_cells, dtype=jnp.int32) * S
    fine = jnp.arange(S, dtype=jnp.int32)
    ca, sa = cos_sin_f32(jnp.mod(coarse[None, :, None] * (spacing * j_index[:, None, :]), G))
    cb, sb = cos_sin_f32(jnp.mod(fine[None, :, None] * (spacing * j_index[:, None, :]), G))
    c1 = (ca[:, :, None, :] * cb[:, None, :, :] - sa[:, :, None, :] * sb[:, None, :, :]).astype(jnp.bfloat16)
    s1 = (sa[:, :, None, :] * cb[:, None, :, :] + ca[:, :, None, :] * sb[:, None, :, :]).astype(jnp.bfloat16)
    c1 = c1.reshape(NF, q_cells, 1, S, 1, j_len)
    s1 = s1.reshape(NF, q_cells, 1, S, 1, j_len)
    ri_in = jnp.arange(2, dtype=jnp.int32).reshape(1, 1, 2, 1, 1, 1)
    ri_out = jnp.arange(2, dtype=jnp.int32).reshape(1, 1, 1, 1, 2, 1)
    w1 = jnp.where(ri_in == ri_out, c1, jnp.where(ri_in == 0, s1, -s1))
    w1 = w1.reshape(NF, q_cells, 2 * S, 2 * j_len)
    transformed = jnp.einsum("raqxk,rqkn->raxn", folded, w1, preferred_element_type=jnp.float32)
    transformed = transformed.astype(jnp.bfloat16).reshape(NF, slab_rows, 2, j_len)

    l_index = jnp.arange(P_SIZE, dtype=jnp.int32) - P_SIZE // 2
    row_base = (tile_index * slab_rows - G // 2) + jnp.arange(row_cells, dtype=jnp.int32) * S
    ca, sa = cos_sin_f32(phase_index(row_base, l_index))
    cb, sb = cos_sin_f32(phase_index(fine, l_index))
    c2 = (ca[:, None, :] * cb[None, :, :] - sa[:, None, :] * sb[None, :, :]).astype(jnp.bfloat16)
    s2 = (sa[:, None, :] * cb[None, :, :] + ca[:, None, :] * sb[None, :, :]).astype(jnp.bfloat16)
    c2 = c2.reshape(slab_rows, P_SIZE)
    s2 = s2.reshape(slab_rows, P_SIZE)
    e2 = jnp.stack([c2, -s2])
    partial = jnp.einsum("iul,ruij->lrj", e2, transformed, preferred_element_type=jnp.float32)
    chan_count = lax.axis_size("chan")
    partial = partial.reshape(chan_count, P_SIZE // chan_count, NF, j_len)
    partial = lax.all_to_all(partial.astype(jnp.bfloat16), "chan", split_axis=0, concat_axis=0, tiled=True)
    partial = jnp.sum(partial.astype(jnp.float32), axis=0)
    partial = partial.reshape(P_SIZE // chan_count, NF, tile_count, j_len // tile_count)
    partial = jnp.transpose(partial, (2, 0, 1, 3))
    partial = lax.all_to_all(partial.astype(jnp.bfloat16), "tile", split_axis=0, concat_axis=0, tiled=True)
    partial = jnp.sum(partial.astype(jnp.float32), axis=0)
    out = jnp.transpose(partial, (0, 2, 1))
    return out.reshape(out.shape[0], -1) * (1.0 / G)


def solution(mesh):
    placed = (
        P("chan", "tile", None),
        P("chan", None, None, None, None),
        P("chan", "tile", None),
        P("chan", "tile"),
        P("chan", "tile"),
    )
    return jax.shard_map(
        local, mesh=mesh, in_specs=placed, out_specs=P("chan", "tile"), check_vma=False
    )
```

profile of v0, /device:TPU:0, one launch (start us, length us, event | category | flops | bytes accessed | tf_op | source)
XLA Modules:
  0.0 535.5 jit_solution(6401761929178297183)
XLA Ops:
  1.3 3.8 sort.17
  5.1 5.0 gather_fusion
  10.9 5.0 gather_fusion.1
  16.7 7.3 %all-to-all-start = ((s32[8,1,96]{2,1,0:T(1,128)}), s32[8,1,96]{2,1,0:T(1,128)S(1)}, u32[]{:S(2)}, u32[]{:S(2)}) async-start(s32[8,1,96]{2,1,0:T(1,128)} %compare_select_fusion.1), calls=%async_computation | async-start | bytes 8192 | tf_op jit(solution)/shard_map/all_to_all | solution.py:69
  42.6 4.6 maximum_bitcast_fusion.4
  49.8 7.6 %broadcast_in_dim.71 = bf16[8,16,2,64,2,128]{5,4,3,2,1,0:T(2,128)(2,1)} broadcast(bf16[8,16,2,64,128]{4,3,2,1,0:T(8,128)(2,1)S(1)} %broadcast_select_fusion), dimensions={0,1,2,3,5} | broadcast | bytes 12582912 | tf_op jit(solution)/shard_map/jit(_where)/broadcast_in_dim | solution.py:114
  57.4 14.0 %broadcast_in_dim.72 = bf16[8,16,128,256]{3,2,1,0:T(8,128)(2,1)} reshape(bf16[8,16,2,64,2,128]{5,4,3,2,1,0:T(2,128)(2,1)} %broadcast_in_dim.71) | data formatting | bytes 16777216 | tf_op jit(solution)/shard_map/jit(_where)/broadcast_in_dim | solution.py:114
  71.4 7.5 %broadcast_in_dim.66 = bf16[8,16,2,64,2,128]{5,4,3,2,1,0:T(2,128)(2,1)} broadcast(bf16[8,16,64,128]{3,2,1,0:T(8,128)(2,1)S(1)} %get-tuple-element.14), dimensions={0,1,3,5} | broadcast | bytes 10485760 | tf_op jit(solution)/shard_map/jit(_where)/broadcast_in_dim | solution.py:114
  78.9 14.0 %broadcast_in_dim.67 = bf16[8,16,128,256]{3,2,1,0:T(8,128)(2,1)} reshape(bf16[8,16,2,64,2,128]{5,4,3,2,1,0:T(2,128)(2,1)} %broadcast_in_dim.66) | data formatting | bytes 16777216 | tf_op jit(solution)/shard_map/jit(_where)/broadcast_in_dim | solution.py:114
  93.7 6.2 %copy.44 = bf16[1024,2,1024]{2,0,1:T(8,128)(2,1)} copy(bf16[1024,2,1024]{0,2,1:T(8,128)(2,1)} %maximum_bitcast_fusion.4) | data formatting | bytes 8388608 | tf_op jit(solution)/shard_map/iul,ruij->lrj/dot_general | solution.py:128
  99.9 6.2 %all-to-all-start.1 = ((f32[8,96,128]{2,1,0:T(8,128)}), f32[8,96,128]{2,1,0:T(8,128)S(1)}, u32[]{:S(2)}, u32[]{:S(2)}) async-start(f32[8,96,128]{2,1,0:T(8,128)} %broadcast_select_fusion.1), calls=%async_computation.1 | async-start | bytes 786432 | tf_op jit(solution)/shard_map/all_to_all | solution.py:68
  106.2 18.0 %gather_fusion.2 = bf16[768,2,64,128]{3,2,1,0:T(8,128)(2,1)} fusion(bf16[32,2,64,128]{3,2,1,0:T(8,128)(2,1)S(1)} %bitcast.101, s32[1024]{0:T(1024)S(1)} %pad_clamp_fusion), kind=kCustom, calls=%fused_computation.2 | custom fusion | bytes 50334720 | tf_op jit(solution)/shard_map/gather | solution.py:83
  124.2 25.6 %fusion.11 = (f32[768,64,128]{2,1,0:T(8,128)}, f32[768,64,128]{2,1,0:T(8,128)}) fusion(bf16[768,2,64,128]{3,2,1,0:T(8,128)(2,1)} %gather_fusion.2), kind=kLoop, calls=%fused_computation.20 | loop fusion | flops 12582912 | bytes 75497472 | tf_op jit(solution)/shard_map/convert_element_type | solution.py:20
  151.4 4.6 multiply_convert_fusion.5
  156.2 31.0 %fusion.76 = (bf16[768,64,64]{2,1,0:T(8,128)(2,1)S(1)}, bf16[768,64,64]{2,1,0:T(8,128)(2,1)}) fusion(f32[768,64,128]{2,1,0:T(8,128)} %get-tuple-element.9, f32[768,64]{1,0:T(8,128)S(1)} %get-tuple-element.16, f32[768,64,128]{2,1,0:T(8,128)} %get-tuple-element.10, f32[768,64]{1,0:T(8,128)S(1)} %get-tuple-element.15), kind=kLoop, calls=%fused_computation.158 | loop fusion | flops 15728640 | bytes 38141952 | tf_op jit(solution)/shard_map/neg | solution.py:29
  187.2 30.3 %subtract_convert_fusion = bf16[768,64,64]{2,1,0:T(8,128)(2,1)} fusion(f32[768,64,128]{2,1,0:T(8,128)} %get-tuple-element.10, f32[768,64,128]{2,1,0:T(8,128)} %get-tuple-element.9, f32[768,64]{1,0:T(8,128)S(1)} %get-tuple-element.16, f32[768,64]{1,0:T(8,128)S(1)} %get-tuple-element.15), kind=kLoop, calls=%fused_computation.15 | loop fusion | flops 12582912 | bytes 31850496 | tf_op jit(solution)/shard_map/convert_element_type | solution.py:22
  217.5 27.7 %maximum_bitcast_fusion.2 = (bf16[768,1,64,128]{3,2,1,0:T(8,128)(2,1)}, bf16[768,1,64,128]{3,2,1,0:T(8,128)(2,1)}) fusion(bf16[768,64,64]{2,1,0:T(8,128)(2,1)} %get-tuple-element.8, bf16[768,64,64]{2,1,0:T(8,128)(2,1)} %subtract_convert_fusion, bf16[768,64,64]{2,1,0:T(8,128)(2,1)S(1)} %get-tuple-element.7), kind=kLoop, calls=%fused_computation.21 | loop fusion | flops 50331648 | bytes 44040192 | tf_op jit(solution)/shard_map/stack | solution.py:26
  245.3 41.6 %fusion.78 = (bf16[768,128,128]{2,1,0:T(8,128)(2,1)}, f32[768,128,128]{2,1,0:T(8,128)}) fusion(bf16[768,2,64,128]{3,2,1,0:T(8,128)(2,1)} %gather_fusion.2, bf16[768,1,64,128]{3,2,1,0:T(8,128)(2,1)} %get-tuple-element.12, bf16[768,1,64,128]{3,2,1,0:T(8,128)(2,1)} %get-tuple-element.11), kind=kOutput, calls=%fused_computation.160 | convolution fusion | flops 3246391296 | bytes 125829120 | tf_op jit(solution)/shard_map/bpkx,bpkn->bxn/dot_general | solution.py:33
  286.9 6.7 %slice.58 = bf16[768,64,64]{2,1,0:T(8,128)(2,1)S(1)} slice(bf16[768,128,128]{2,1,0:T(8,128)(2,1)} %get-tuple-element.30), slice={[0:768], [0:64], [0:64]} | slice | bytes 12582912 | tf_op jit(solution)/shard_map/slice | solution.py:84
  293.5 5.3 copy-done.2
  298.8 5.2 slice.56
  304.0 12.0 %fusion = bf16[768,64,64]{2,1,0:T(8,128)(2,1)S(1)} fusion(f32[768,128,128]{2,1,0:T(8,128)} %get-tuple-element.31), kind=kLoop, calls=%fused_computation.6 | loop fusion | flops 6291456 | bytes 18874368 | tf_op jit(solution)/shard_map/convert.6
  316.0 8.7 %pad_maximum_fusion = bf16[768,64,128]{2,1,0:T(8,128)(2,1)} fusion(bf16[768,64,64]{2,1,0:T(8,128)(2,1)S(1)} %slice.58, bf16[768,64,64]{2,1,0:T(8,128)(2,1)S(1)} %fusion), kind=kLoop, calls=%fused_computation.23 | loop fusion | flops 25165824 | bytes 25165824 | tf_op jit(solution)/shard_map/concatenate | solution.py:84
  324.7 19.3 %stack.33 = bf16[768,1,8192]{2,0,1:T(8,128)(2,1)} reshape(bf16[768,64,128]{2,1,0:T(8,128)(2,1)} %pad_maximum_fusion) | data formatting | bytes 25165824 | tf_op jit(solution)/shard_map/stack | solution.py:85
  344.0 19.3 %stack.32 = bf16[768,1,8192]{2,0,1:T(8,128)(2,1)} reshape(bf16[768,64,128]{2,1,0:T(8,128)(2,1)} %slice.56) | data formatting | bytes 25165824 | tf_op jit(solution)/shard_map/stack | solution.py:85
  363.3 59.6 %bitcast_convert_fusion = bf16[8,16,16,8192]{3,2,1,0:T(8,128)(2,1)} fusion(bf16[768,1,8192]{2,0,1:T(8,128)(2,1)} %stack.33, bf16[768,1,8192]{2,0,1:T(8,128)(2,1)} %stack.32, bf16[8,16,16,768,2]{3,2,4,1,0:T(8,128)(2,1)} %multiply_convert_fusion.5), kind=kOutput, calls=%fused_computation.4 | convolution fusion | flops 51568967680 | bytes 65011712 | tf_op jit(solution)/shard_map/raqsk,skn->raqn/dot_general | solution.py:100
  422.9 23.1 %copy.68 = bf16[256,8,64,128]{3,2,1,0:T(8,128)(2,1)} copy(bf16[256,8,64,128]{3,1,2,0:T(8,128)(2,1)} %bitcast.105) | data formatting | bytes 67108864
  446.0 21.1 %bitcast_convert_fusion.1 = bf16[8,16,64,256]{3,2,1,0:T(8,128)(2,1)} fusion(bf16[8,16,16,64,128]{4,3,2,1,0:T(8,128)(2,1)} %bitcast.104, bf16[8,16,128,256]{3,2,1,0:T(8,128)(2,1)} %broadcast_in_dim.67, bf16[8,16,128,256]{3,2,1,0:T(8,128)(2,1)} %broadcast_in_dim.72, pred[128,256]{1,0:T(8,128)(4,1)S(1)} %bitcast.115), kind=kOutput, calls=%fused_computation.27 | convolution fusion | flops 8596226048 | bytes 54558720 | tf_op jit(solution)/shard_map/raqxk,rqkn->raxn/dot_general | solution.py:116
  467.0 7.2 %reshape.827 = bf16[8,1024,2,128]{3,2,1,0:T(2,128)(2,1)} reshape(bf16[8,16,64,256]{3,2,1,0:T(8,128)(2,1)} %bitcast_convert_fusion.1) | data formatting | bytes 8388608 | tf_op jit(solution)/shard_map/reshape | solution.py:117
  474.2 8.0 %bitcast_convert_fusion.2 = bf16[4,256,8,128]{3,1,2,0:T(8,128)(2,1)S(1)} fusion(bf16[8,1024,2,128]{3,2,1,0:T(2,128)(2,1)} %reshape.827, bf16[4,256,2,1024,1]{3,1,0,2,4:T(8,128)(2,1)} %bitcast.108), kind=kOutput, calls=%fused_computation.33 | convolution fusion | flops 4296015872 | bytes 10485760 | tf_op jit(solution)/shard_map/iul,ruij->lrj/dot_general | solution.py:128
  482.2 28.3 %all_to_all.21 = bf16[4,256,8,128]{3,1,2,0:T(8,128)(2,1)S(1)} all-to-all(bf16[4,256,8,128]{3,1,2,0:T(8,128)(2,1)S(1)} %bitcast_convert_fusion.2), channel_id=1, replica_groups=mesh['tile'=8,'chan'=4] {'chan'}, dimensions={0} | all-to-all | bytes 4194304 | tf_op jit(solution)/shard_map/all_to_all | solution.py:131
  513.0 21.1 %all_to_all.22 = bf16[8,256,8,16]{1,3,2,0:T(8,128)(2,1)S(1)} all-to-all(bf16[8,256,8,16]{1,3,2,0:T(8,128)(2,1)S(1)} %copy.52), channel_id=1, replica_groups=mesh['tile'=8,'chan'=4] {'tile'}, dimensions={0} | all-to-all | bytes 1048576 | tf_op jit(solution)/shard_map/all_to_all | solution.py:135
  (68 shorter events, 30.1 us)
Async XLA Ops:
  0.0 106.2 %copy-start = (bf16[1,32,2,64,128]{4,3,2,1,0:T(8,128)(2,1)S(1)}, bf16[1,32,2,64,128]{4,3,2,1,0:T(8,128)(2,1)}, u32[]{:S(2)}) copy-start(bf16[1,32,2,64,128]{4,3,2,1,0:T(8,128)(2,1)} %param.6) | copy-start | bytes 3145732
  0.0 38.4 %copy-start.3 = (f32[1,256,128]{2,1,0:T(8,128)S(1)}, f32[1,256,128]{2,1,0:T(8,128)}, u32[]{:S(2)}) copy-start(f32[1,256,128]{2,1,0:T(8,128)} %param.5) | copy-start | bytes 393220
  16.7 83.2 %all-to-all-start = ((s32[8,1,96]{2,1,0:T(1,128)}), s32[8,1,96]{2,1,0:T(1,128)S(1)}, u32[]{:S(2)}, u32[]{:S(2)}) async-start(s32[8,1,96]{2,1,0:T(1,128)} %compare_select_fusion.1), calls=%async_computation | async-start | bytes 8192 | tf_op jit(solution)/shard_map/all_to_all | solution.py:69
  32.5 14.7 %copy-start.5 = (pred[2]{0:T(512)(128)(4,1)S(1)}, pred[2]{0:T(512)(128)(4,1)}, u32[]{:S(2)}) copy-start(pred[2]{0:T(512)(128)(4,1)} %iota_compare_fusion.5) | copy-start | bytes 10
  99.9 56.1 %all-to-all-start.1 = ((f32[8,96,128]{2,1,0:T(8,128)}), f32[8,96,128]{2,1,0:T(8,128)S(1)}, u32[]{:S(2)}, u32[]{:S(2)}) async-start(f32[8,96,128]{2,1,0:T(8,128)} %broadcast_select_fusion.1), calls=%async_computation.1 | async-start | bytes 786432 | tf_op jit(solution)/shard_map/all_to_all | solution.py:68
  286.9 12.0 %copy-start.2 = (bf16[768,128,128]{2,1,0:T(8,128)(2,1)S(1)}, bf16[768,128,128]{2,1,0:T(8,128)(2,1)}, u32[]{:S(2)}) copy-start(bf16[768,128,128]{2,1,0:T(8,128)(2,1)} %get-tuple-element.30) | copy-start | bytes 75497472
  422.9 23.1 %copy-start.4 = (pred[16,8,2,128]{3,1,2,0:T(8,128)(4,1)S(1)}, pred[16,8,2,128]{3,1,2,0:T(8,128)(4,1)}, u32[]{:S(2)}) copy-start(pred[16,8,2,128]{3,1,2,0:T(8,128)(4,1)} %copy.83) | copy-start | bytes 98308
  474.2 60.9 %copy-start.1 = (bf16[1,32,2,64,128]{4,3,2,1,0:T(8,128)(2,1)S(1)}, bf16[1,32,2,64,128]{4,3,2,1,0:T(8,128)(2,1)}, u32[]{:S(2)}) copy-start(bf16[1,32,2,64,128]{4,3,2,1,0:T(8,128)(2,1)} %param.6) | copy-start | bytes 3145732
where the time goes:
time: 545 us; the launch traced here: 536 us
  other arithmetic  172 us (32%)
  local copies, waits for them, and re-layouts  170 us (31%)
  matrix products  130 us (24%)
  blocking collectives  49.4 us (9%)
  starting transfers between devices  13.5 us (2%)
    dot_general x1, matrix products, local(): jnp.einsum('raqsk,skn->raqn', l2, p2, preferred_element_type=jnp.float32)  59.6 us
    broadcast_in_dim x5, local copies, waits for them, and re-layouts, local(): w1 = jnp.where(ri_in == ri_out, c1, jnp.where(ri_in == 0, s1, -s1))  43.3 us
    dot_general x1, matrix products, block_patches(): jnp.einsum('bpkx,bpkn->bxn', kernel_rows, v_weighted, preferred_element_t...  41.6 us
    another operation x2, local copies, waits for them, and re-layouts, local(): jnp.stack([patches, rotated], axis=1).astype(jnp.bfloat16)  38.6 us
    neg x1, other arithmetic, block_patches(): -weighted_imag  31 us
    convert_element_type x1, other arithmetic, block_patches(): (vis_real * kern_real - vis_imag * kern_imag).astype(jnp.bfloat16)  30.3 us
    unnamed x14, local copies, waits for them, and re-layouts  29.1 us
    all_to_all x1, blocking collectives, local(): lax.all_to_all(partial.astype(jnp.bfloat16), 'chan', split_axis=0, concat...  28.3 us
  transfers between devices with their start and end apart: 2, of which 0 were waited for; matrix products, arithmetic and copies ran while one was open for 23% of the time, Pallas kernels for 0%

commit v1 on v0

--- a/solution.py
+++ b/solution.py
@@ -4,6 +4,8 @@
 import jax.numpy as jnp
 from jax import lax
 from jax.sharding import PartitionSpec as P
+from jax.experimental import pallas as pl
+from jax.experimental.pallas import tpu as pltpu
 
 G = 8192
 S = 64
@@ -32,6 +34,54 @@
     )
     patch = jnp.einsum("bpkx,bpkn->bxn", kernel_rows, v_weighted, preferred_element_type=jnp.float32)
     return patch[:, :support, :]
+
+
+PATCH_CHUNK = 128
+
+
+def patch_kernel(plane_ref, samples_ref, u_ref, v_ref, out_ref):
+    base = pl.program_id(0) * PATCH_CHUNK
+    lane = lax.broadcasted_iota(jnp.int32, (S, 2 * S), 1)
+    low = lane < S
+    sign = jnp.where(low, -1.0, 1.0).astype(jnp.float32)
+    for j in range(PATCH_CHUNK):
+        w = plane_ref[base + j]
+        column = samples_ref[:, j : j + 1]
+        vis_real = column[:S]
+        vis_imag = column[S:]
+        kern_real = v_ref[w, 0].astype(jnp.float32)
+        kern_imag = v_ref[w, 1].astype(jnp.float32)
+        w_real = (vis_real * kern_real - vis_imag * kern_imag).astype(jnp.bfloat16).astype(jnp.float32)
+        w_imag = (vis_real * kern_imag + vis_imag * kern_real).astype(jnp.bfloat16).astype(jnp.float32)
+        top = jnp.where(low, pltpu.roll(w_real, S, 1), w_imag)
+        bottom = jnp.where(low, -pltpu.roll(w_imag, S, 1), w_real)
+        rhs = jnp.concatenate([top, bottom], axis=0).astype(jnp.bfloat16)
+        patch = jnp.dot(u_ref[w], rhs, preferred_element_type=jnp.float32)
+        out_ref[j, 0] = patch.astype(jnp.bfloat16)
+        out_ref[j, 1] = (pltpu.roll(patch, S, 1) * sign).astype(jnp.bfloat16)
+
+
+def patches_rotated(samples, planes, kernel_set):
+    slots = samples.shape[0]
+    u_kernel = jnp.transpose(kernel_set[:, :, :, :S], (0, 3, 1, 2)).reshape(NW, S, 2 * S)
+    grid_spec = pltpu.PrefetchScalarGridSpec(
+        num_scalar_prefetch=1,
+        grid=(slots // PATCH_CHUNK,),
+        in_specs=[
+            pl.BlockSpec((2 * S, PATCH_CHUNK), lambda i, p: (0, i)),
+            pl.BlockSpec((NW, S, 2 * S), lambda i, p: (0, 0, 0)),
+            pl.BlockSpec((NW, 2, S, 2 * S), lambda i, p: (0, 0, 0, 0)),
+        ],
+        out_specs=pl.BlockSpec((PATCH_CHUNK, 2, S, 2 * S), lambda i, p: (i, 0, 0, 0)),
+    )
+    return pl.pallas_call(
+        patch_kernel,
+        grid_spec=grid_spec,
+        out_shape=jax.ShapeDtypeStruct((slots, 2, S, 2 * S), jnp.bfloat16),
+        cost_estimate=pl.CostEstimate(
+            flops=2 * slots * S * 2 * S * 2 * S, transcendentals=0, bytes_accessed=slots * 2 * S * 2 * S * 2 * 2
+        ),
+    )(planes, jnp.transpose(samples), u_kernel, kernel_set)
 
 
 def phase_index(rows, cols):
@@ -80,9 +130,7 @@
 
     cell_r = arrived_meta // NW
     plane_r = arrived_meta % NW
-    patches = block_patches(arrived, kernel_set[plane_r])
-    rotated = jnp.concatenate([-patches[:, :, S:], patches[:, :, :S]], axis=-1)
-    p2 = jnp.stack([patches, rotated], axis=1).astype(jnp.bfloat16).reshape(slot_total, 2, S * 2 * S)
+    p2 = patches_rotated(arrived, plane_r, kernel_set).reshape(slot_total, 2, S * 2 * S)
 
     a_s = cell_r // cell_cols
     cc_s = cell_r % cell_cols

time: 545 us -> 529 us (0.971); the launches traced: 536 us -> 527 us
  Pallas kernels: 0 us -> 209 us
  other arithmetic: 172 us -> 31.5 us
  matrix products: 130 us -> 90.3 us
  local copies, waits for them, and re-layouts: 170 us -> 132 us
    pallas_call x0 -> x1, Pallas kernels: none -> 209 us  [patches_rotated(): pl.pallas_call(patch_kernel, grid_spec=grid_spec, out_shape=jax.ShapeDtyp...]
    convert_element_type x2 -> x0, other arithmetic: 55.9 us -> none  [the longest x1 30.3 us: block_patches(): (vis_real * kern_real - vis_imag * kern_imag).astype(jnp.bfloat16)]
    dot_general x1 -> x0, matrix products: 41.6 us -> none  [block_patches(): jnp.einsum('bpkx,bpkn->bxn', kernel_rows, v_weighted, preferred_element_t...]
    another operation x3 -> x1, other arithmetic: 39.9 us -> 0.18 us  [the longest x1 27.7 us: block_patches(): jnp.stack([jnp.concatenate([weighted_real, weighted_imag], axis=-1), jnp....]
    another operation x2 -> x0, local copies, waits for them, and re-layouts: 38.6 us -> none  [local(): jnp.stack([patches, rotated], axis=1).astype(jnp.bfloat16)]
    reshape x0 -> x3, local copies, waits for them, and re-layouts: none -> 36.8 us  [the longest x1 34.7 us: local(): patches_rotated(arrived, plane_r, kernel_set)]
    neg x1 -> x0, other arithmetic: 31 us -> none  [block_patches(): -weighted_imag]
    gather x1 -> x0, local copies, waits for them, and re-layouts: 18 us -> none  [local(): patches = block_patches(arrived, kernel_set[plane_r])]
  transfers between devices with their start and end apart: 2 -> 2, of which waited for: 0 -> 1; matrix products, arithmetic and copies ran while one was open for 23% -> 15% of each run, Pallas kernels for 0% -> 0%
where the time goes in v1:
time: 529 us; the launch traced here: 527 us
  Pallas kernels  209 us (40%)
  local copies, waits for them, and re-layouts  132 us (25%)
  matrix products  90.3 us (17%)
  blocking collectives  46 us (9%)
  other arithmetic  31.5 us (6%)
  starting transfers between devices  13.3 us (3%)
    pallas_call x1, Pallas kernels, patches_rotated(): pl.pallas_call(patch_kernel, grid_spec=grid_spec, out_shape=jax.ShapeDtyp...  209 us
    dot_general x1, matrix products, local(): jnp.einsum('raqsk,skn->raqn', l2, p2, preferred_element_type=jnp.float32)  61.3 us
    broadcast_in_dim x5, local copies, waits for them, and re-layouts, local(): w1 = jnp.where(ri_in == ri_out, c1, jnp.where(ri_in == 0, s1, -s1))  44.5 us
    reshape x1, local copies, waits for them, and re-layouts, local(): patches_rotated(arrived, plane_r, kernel_set)  34.7 us
    all_to_all x1, blocking collectives, local(): lax.all_to_all(partial.astype(jnp.bfloat16), 'chan', split_axis=0, concat...  28.4 us
    unnamed x18, local copies, waits for them, and re-layouts  23.7 us
    dot_general x1, matrix products, local(): jnp.einsum('raqxk,rqkn->raxn', folded, w1, preferred_element_type=jnp.flo...  21.1 us
    all_to_all x1, blocking collectives, local(): lax.all_to_all(partial.astype(jnp.bfloat16), 'tile', split_axis=0, concat...  17.6 us
  transfers between devices with their start and end apart: 2, of which 1 were waited for; matrix products, arithmetic and copies ran while one was open for 15% of the time, Pallas kernels for 0%

profile of v1, /device:TPU:0, one launch (start us, length us, event | category | flops | bytes accessed | tf_op | source)
XLA Modules:
  0.0 526.6 jit_solution(4412013709375472709)
XLA Ops:
  1.2 3.8 sort.17
  5.0 5.0 gather_fusion
  10.2 5.0 gather_fusion.1
  16.0 7.3 %all-to-all-start = ((s32[8,1,96]{2,1,0:T(1,128)}), s32[8,1,96]{2,1,0:T(1,128)S(1)}, u32[]{:S(2)}, u32[]{:S(2)}) async-start(s32[8,1,96]{2,1,0:T(1,128)} %compare_select_fusion), calls=%async_computation | async-start | bytes 8192 | tf_op jit(solution)/shard_map/all_to_all | solution.py:119
  23.3 1.0 fusion.31
  24.7 2.5 add_convert_fusion
  27.2 2.0 fusion.60
  29.2 1.0 fusion.33
  30.6 2.0 subtract_convert_fusion.1
  32.6 2.0 fusion.13
  34.6 1.6 gather_fusion.2
  37.1 4.7 maximum_bitcast_fusion
  41.8 2.3 broadcast_select_fusion
  44.2 1.1 copy.48.u_ref
  45.3 8.8 %broadcast_in_dim.80 = bf16[8,16,2,64,2,128]{5,4,3,2,1,0:T(2,128)(2,1)} broadcast(bf16[8,16,2,64,128]{4,3,2,1,0:T(8,128)(2,1)} %broadcast_select_fusion), dimensions={0,1,2,3,5} | broadcast | bytes 12582912 | tf_op jit(solution)/shard_map/jit(_where)/broadcast_in_dim | solution.py:162
  54.1 14.1 %broadcast_in_dim.81 = bf16[8,16,128,256]{3,2,1,0:T(8,128)(2,1)} reshape(bf16[8,16,2,64,2,128]{5,4,3,2,1,0:T(2,128)(2,1)} %broadcast_in_dim.80) | data formatting | bytes 16777216 | tf_op jit(solution)/shard_map/jit(_where)/broadcast_in_dim | solution.py:162
  68.1 7.5 %broadcast_in_dim.66 = bf16[8,16,2,64,2,128]{5,4,3,2,1,0:T(2,128)(2,1)} broadcast(bf16[8,16,64,128]{3,2,1,0:T(8,128)(2,1)S(1)} %get-tuple-element.8), dimensions={0,1,3,5} | broadcast | bytes 10485760 | tf_op jit(solution)/shard_map/jit(_where)/broadcast_in_dim | solution.py:162
  75.7 14.1 %broadcast_in_dim.67 = bf16[8,16,128,256]{3,2,1,0:T(8,128)(2,1)} reshape(bf16[8,16,2,64,2,128]{5,4,3,2,1,0:T(2,128)(2,1)} %broadcast_in_dim.66) | data formatting | bytes 16777216 | tf_op jit(solution)/shard_map/jit(_where)/broadcast_in_dim | solution.py:162
  90.5 6.2 %copy.45 = bf16[1024,2,1024]{2,0,1:T(8,128)(2,1)} copy(bf16[1024,2,1024]{0,2,1:T(8,128)(2,1)} %maximum_bitcast_fusion) | data formatting | bytes 8388608 | tf_op jit(solution)/shard_map/iul,ruij->lrj/dot_general | solution.py:176
  96.7 6.0 %all-to-all-start.1 = ((f32[8,96,128]{2,1,0:T(8,128)}), f32[8,96,128]{2,1,0:T(8,128)S(1)}, u32[]{:S(2)}, u32[]{:S(2)}) async-start(f32[8,96,128]{2,1,0:T(8,128)} %broadcast_select_fusion.1), calls=%async_computation.1 | async-start | bytes 786432 | tf_op jit(solution)/shard_map/all_to_all | solution.py:118
  104.9 4.6 multiply_convert_fusion.4
  109.5 4.4 all-to-all-done.1
  113.8 0.9 copy.47
  114.7 209.3 %shard_map.55 = bf16[768,2,64,128]{3,2,1,0:T(8,128)(2,1)} custom-call(s32[768]{0:T(1024)} %get-tuple-element.20.plane_ref, f32[128,768]{1,0:T(8,128)} %bitcast.87, bf16[32,64,128]{2,1,0:T(8,128)(2,1)} %copy.48.u_ref, bf16[32,2,64,128]{3,2,1,0:T(8,128)(2,1)} %bitcast.81), custom_call_target="tpu_custom_call" | custom-call | flops 1610612736 | bytes 50331648 | tf_op jit(solution)/shard_map/pallas_call | solution.py:77
  324.0 34.7 %reshape.756 = bf16[768,2,8192]{2,1,0:T(2,128)(2,1)} reshape(bf16[768,2,64,128]{3,2,1,0:T(8,128)(2,1)} %shard_map.55) | data formatting | bytes 50331648 | tf_op jit(solution)/shard_map/reshape | solution.py:133
  358.7 61.3 %bitcast_convert_fusion = bf16[8,16,16,8192]{3,2,1,0:T(8,128)(2,1)} fusion(bf16[768,2,8192,1,1]{2,1,0,4,3:T(2,128)(2,1)} %bitcast.78, bf16[8,16,16,768,2]{3,2,4,1,0:T(8,128)(2,1)} %multiply_convert_fusion.4), kind=kOutput, calls=%fused_computation.3 | convolution fusion | flops 51556384768 | bytes 65011712 | tf_op jit(solution)/shard_map/raqsk,skn->raqn/dot_general | solution.py:148
  420.0 23.1 %copy.68 = bf16[256,8,64,128]{3,2,1,0:T(8,128)(2,1)} copy(bf16[256,8,64,128]{3,1,2,0:T(8,128)(2,1)} %bitcast.77) | data formatting | bytes 67108864
  443.1 21.1 %bitcast_convert_fusion.1 = bf16[8,16,64,256]{3,2,1,0:T(8,128)(2,1)} fusion(bf16[8,16,16,64,128]{4,3,2,1,0:T(8,128)(2,1)} %bitcast.76, bf16[8,16,128,256]{3,2,1,0:T(8,128)(2,1)} %broadcast_in_dim.67, bf16[8,16,128,256]{3,2,1,0:T(8,128)(2,1)} %broadcast_in_dim.81, pred[128,256]{1,0:T(8,128)(4,1)S(1)} %bitcast.90), kind=kOutput, calls=%fused_computation.8 | convolution fusion | flops 8596226048 | bytes 54558720 | tf_op jit(solution)/shard_map/raqxk,rqkn->raxn/dot_general | solution.py:164
  464.1 6.9 %reshape.758 = bf16[8,1024,2,128]{3,2,1,0:T(2,128)(2,1)} reshape(bf16[8,16,64,256]{3,2,1,0:T(8,128)(2,1)} %bitcast_convert_fusion.1) | data formatting | bytes 8388608 | tf_op jit(solution)/shard_map/reshape | solution.py:165
  471.1 7.9 %bitcast_convert_fusion.2 = bf16[4,256,8,128]{3,1,2,0:T(8,128)(2,1)S(1)} fusion(bf16[8,1024,2,128]{3,2,1,0:T(2,128)(2,1)} %reshape.758, bf16[4,256,2,1024,1]{3,1,0,2,4:T(8,128)(2,1)} %bitcast.83), kind=kOutput, calls=%fused_computation.14 | convolution fusion | flops 4296015872 | bytes 10485760 | tf_op jit(solution)/shard_map/iul,ruij->lrj/dot_general | solution.py:176
  479.0 28.4 %all_to_all.21 = bf16[4,256,8,128]{3,1,2,0:T(8,128)(2,1)S(1)} all-to-all(bf16[4,256,8,128]{3,1,2,0:T(8,128)(2,1)S(1)} %bitcast_convert_fusion.2), channel_id=1, replica_groups=mesh['tile'=8,'chan'=4] {'chan'}, dimensions={0} | all-to-all | bytes 4194304 | tf_op jit(solution)/shard_map/all_to_all | solution.py:179
  508.1 17.6 %all_to_all.22 = bf16[8,256,8,16]{1,3,2,0:T(8,128)(2,1)S(1)} all-to-all(bf16[8,256,8,16]{1,3,2,0:T(8,128)(2,1)S(1)} %copy.53), channel_id=1, replica_groups=mesh['tile'=8,'chan'=4] {'tile'}, dimensions={0} | all-to-all | bytes 1048576 | tf_op jit(solution)/shard_map/all_to_all | solution.py:183
  (60 shorter events, 8.2 us)
Async XLA Ops:
  0.0 34.6 %copy-start = (f32[1,256,128]{2,1,0:T(8,128)S(1)}, f32[1,256,128]{2,1,0:T(8,128)}, u32[]{:S(2)}) copy-start(f32[1,256,128]{2,1,0:T(8,128)} %param.5) | copy-start | bytes 393220
  0.0 10.2 %copy-start.7 = (s32[1,256]{1,0:T(1,128)S(1)}, s32[1,256]{1,0:T(1,128)}, u32[]{:S(2)}) copy-start(s32[1,256]{1,0:T(1,128)} %param.8) | copy-start | bytes 3076
  0.0 10.2 %copy-start.6 = (s32[1,256]{1,0:T(1,128)S(1)}, s32[1,256]{1,0:T(1,128)}, u32[]{:S(2)}) copy-start(s32[1,256]{1,0:T(1,128)} %param.9) | copy-start | bytes 3076
  16.0 80.7 %all-to-all-start = ((s32[8,1,96]{2,1,0:T(1,128)}), s32[8,1,96]{2,1,0:T(1,128)S(1)}, u32[]{:S(2)}, u32[]{:S(2)}) async-start(s32[8,1,96]{2,1,0:T(1,128)} %compare_select_fusion), calls=%async_computation | async-start | bytes 8192 | tf_op jit(solution)/shard_map/all_to_all | solution.py:119
  37.1 4.7 copy-start.2
  37.1 4.7 copy-start.3
  41.8 2.3 copy-start.4
  96.7 17.1 %all-to-all-start.1 = ((f32[8,96,128]{2,1,0:T(8,128)}), f32[8,96,128]{2,1,0:T(8,128)S(1)}, u32[]{:S(2)}, u32[]{:S(2)}) async-start(f32[8,96,128]{2,1,0:T(8,128)} %broadcast_select_fusion.1), calls=%async_computation.1 | async-start | bytes 786432 | tf_op jit(solution)/shard_map/all_to_all | solution.py:118
  420.0 23.1 %copy-start.5 = (pred[16,8,2,128]{3,1,2,0:T(8,128)(4,1)S(1)}, pred[16,8,2,128]{3,1,2,0:T(8,128)(4,1)}, u32[]{:S(2)}) copy-start(pred[16,8,2,128]{3,1,2,0:T(8,128)(4,1)} %copy.86) | copy-start | bytes 98308
  479.0 47.6 %copy-start.1 = (f32[1,256,128]{2,1,0:T(8,128)S(1)}, f32[1,256,128]{2,1,0:T(8,128)}, u32[]{:S(2)}) copy-start(f32[1,256,128]{2,1,0:T(8,128)} %param.5) | copy-start | bytes 393220

commit v2 on v1

--- a/solution.py
+++ b/solution.py
@@ -41,29 +41,31 @@
 
 def patch_kernel(plane_ref, samples_ref, u_ref, v_ref, out_ref):
     base = pl.program_id(0) * PATCH_CHUNK
-    lane = lax.broadcasted_iota(jnp.int32, (S, 2 * S), 1)
-    low = lane < S
-    sign = jnp.where(low, -1.0, 1.0).astype(jnp.float32)
     for j in range(PATCH_CHUNK):
         w = plane_ref[base + j]
         column = samples_ref[:, j : j + 1]
         vis_real = column[:S]
         vis_imag = column[S:]
-        kern_real = v_ref[w, 0].astype(jnp.float32)
-        kern_imag = v_ref[w, 1].astype(jnp.float32)
-        w_real = (vis_real * kern_real - vis_imag * kern_imag).astype(jnp.bfloat16).astype(jnp.float32)
-        w_imag = (vis_real * kern_imag + vis_imag * kern_real).astype(jnp.bfloat16).astype(jnp.float32)
-        top = jnp.where(low, pltpu.roll(w_real, S, 1), w_imag)
-        bottom = jnp.where(low, -pltpu.roll(w_imag, S, 1), w_real)
-        rhs = jnp.concatenate([top, bottom], axis=0).astype(jnp.bfloat16)
-        patch = jnp.dot(u_ref[w], rhs, preferred_element_type=jnp.float32)
-        out_ref[j, 0] = patch.astype(jnp.bfloat16)
-        out_ref[j, 1] = (pltpu.roll(patch, S, 1) * sign).astype(jnp.bfloat16)
+        first = v_ref[w, 0].astype(jnp.float32)
+        second = v_ref[w, 1].astype(jnp.float32)
+        top = (vis_real * first + vis_imag * second).astype(jnp.bfloat16)
+        bottom = (vis_real * second - vis_imag * first).astype(jnp.bfloat16)
+        rhs = jnp.concatenate(
+            [jnp.concatenate([top, bottom], axis=1), jnp.concatenate([bottom, -top], axis=1)], axis=0
+        )
+        both = jnp.dot(u_ref[w], rhs, preferred_element_type=jnp.float32)
+        out_ref[j, 0] = both[:, : 2 * S].astype(jnp.bfloat16)
+        out_ref[j, 1] = both[:, 2 * S :].astype(jnp.bfloat16)
 
 
 def patches_rotated(samples, planes, kernel_set):
     slots = samples.shape[0]
     u_kernel = jnp.transpose(kernel_set[:, :, :, :S], (0, 3, 1, 2)).reshape(NW, S, 2 * S)
+    v_real = kernel_set[:, 0, :, S:]
+    v_imag = kernel_set[:, 1, :, S:]
+    v_parts = jnp.stack(
+        [jnp.concatenate([v_real, v_imag], axis=-1), jnp.concatenate([-v_imag, v_real], axis=-1)], axis=1
+    )
     grid_spec = pltpu.PrefetchScalarGridSpec(
         num_scalar_prefetch=1,
         grid=(slots // PATCH_CHUNK,),
@@ -79,9 +81,9 @@
         grid_spec=grid_spec,
         out_shape=jax.ShapeDtypeStruct((slots, 2, S, 2 * S), jnp.bfloat16),
         cost_estimate=pl.CostEstimate(
-            flops=2 * slots * S * 2 * S * 2 * S, transcendentals=0, bytes_accessed=slots * 2 * S * 2 * S * 2 * 2
+            flops=2 * slots * S * 2 * S * 4 * S, transcendentals=0, bytes_accessed=slots * 2 * S * 2 * S * 2 * 2
         ),
-    )(planes, jnp.transpose(samples), u_kernel, kernel_set)
+    )(planes, jnp.transpose(samples), u_kernel, v_parts)
 
 
 def phase_index(rows, cols):
@@ -153,14 +155,15 @@
     fine = jnp.arange(S, dtype=jnp.int32)
     ca, sa = cos_sin_f32(jnp.mod(coarse[None, :, None] * (spacing * j_index[:, None, :]), G))
     cb, sb = cos_sin_f32(jnp.mod(fine[None, :, None] * (spacing * j_index[:, None, :]), G))
-    c1 = (ca[:, :, None, :] * cb[:, None, :, :] - sa[:, :, None, :] * sb[:, None, :, :]).astype(jnp.bfloat16)
-    s1 = (sa[:, :, None, :] * cb[:, None, :, :] + ca[:, :, None, :] * sb[:, None, :, :]).astype(jnp.bfloat16)
-    c1 = c1.reshape(NF, q_cells, 1, S, 1, j_len)
-    s1 = s1.reshape(NF, q_cells, 1, S, 1, j_len)
-    ri_in = jnp.arange(2, dtype=jnp.int32).reshape(1, 1, 2, 1, 1, 1)
-    ri_out = jnp.arange(2, dtype=jnp.int32).reshape(1, 1, 1, 1, 2, 1)
+    ca = jnp.tile(ca, (1, 1, 2))[:, :, None, :]
+    sa = jnp.tile(sa, (1, 1, 2))[:, :, None, :]
+    cb = jnp.tile(cb, (1, 2, 2))[:, None, :, :]
+    sb = jnp.tile(sb, (1, 2, 2))[:, None, :, :]
+    c1 = (ca * cb - sa * sb).astype(jnp.bfloat16)
+    s1 = (sa * cb + ca * sb).astype(jnp.bfloat16)
+    ri_in = lax.broadcasted_iota(jnp.int32, (1, 1, 2 * S, 2 * j_len), 2) // S
+    ri_out = lax.broadcasted_iota(jnp.int32, (1, 1, 2 * S, 2 * j_len), 3) // j_len
     w1 = jnp.where(ri_in == ri_out, c1, jnp.where(ri_in == 0, s1, -s1))
-    w1 = w1.reshape(NF, q_cells, 2 * S, 2 * j_len)
     transformed = jnp.einsum("raqxk,rqkn->raxn", folded, w1, preferred_element_type=jnp.float32)
     transformed = transformed.astype(jnp.bfloat16).reshape(NF, slab_rows, 2, j_len)
 

time: 529 us -> 303 us (0.57)
  Pallas kernels: 209 us -> 20 us
  local copies, waits for them, and re-layouts: 132 us -> 96.3 us
    pallas_call x1, Pallas kernels: 209 us -> 20 us  [patches_rotated(): pl.pallas_call(patch_kernel, grid_spec=grid_spec, out_shape=jax.ShapeDtyp...]
    broadcast_in_dim x5 -> x0, local copies, waits for them, and re-layouts: 44.5 us -> none  [local(): w1 = jnp.where(ri_in == ri_out, c1, jnp.where(ri_in == 0, s1, -s1))]
    another operation x0 -> x8, local copies, waits for them, and re-layouts: none -> 6.15 us  [the longest x2 2.31 us: local(): sb = jnp.tile(sb, (1, 2, 2))[:, None, :, :]]
    unnamed x18 -> x44, local copies, waits for them, and re-layouts: 23.7 us -> 23.4 us
  transfers between devices with their start and end apart: 2 -> 2, of which waited for: 1 -> 1; matrix products, arithmetic and copies ran while one was open for 15% -> 16% of each run, Pallas kernels for 0% -> 0%
where the time goes in v2:
time: 303 us; the launch traced here: 302 us
  local copies, waits for them, and re-layouts  96.3 us (32%)
  matrix products  85.7 us (28%)
  blocking collectives  46 us (15%)
  other arithmetic  35.6 us (12%)
  Pallas kernels  20 us (7%)
  starting transfers between devices  13.3 us (4%)
  waiting for transfers between devices  4.37 us (1%)
    dot_general x1, matrix products, local(): jnp.einsum('raqsk,skn->raqn', l2, p2, preferred_element_type=jnp.float32)  61.3 us
    reshape x1, local copies, waits for them, and re-layouts, local(): patches_rotated(arrived, plane_r, kernel_set)  34.8 us
    all_to_all x1, blocking collectives, local(): lax.all_to_all(partial.astype(jnp.bfloat16), 'chan', split_axis=0, concat...  28.4 us
    unnamed x44, local copies, waits for them, and re-layouts  23.4 us
    pallas_call x1, Pallas kernels, patches_rotated(): pl.pallas_call(patch_kernel, grid_spec=grid_spec, out_shape=jax.ShapeDtyp...  20 us
    all_to_all x1, blocking collectives, local(): lax.all_to_all(partial.astype(jnp.bfloat16), 'tile', split_axis=0, concat...  17.6 us
    dot_general x1, matrix products, local(): jnp.einsum('raqxk,rqkn->raxn', folded, w1, preferred_element_type=jnp.flo...  16.4 us
    dot_general x1, matrix products, local(): jnp.einsum('iul,ruij->lrj', e2, transformed, preferred_element_type=jnp.f...  7.95 us
  transfers between devices with their start and end apart: 2, of which 1 were waited for; matrix products, arithmetic and copies ran while one was open for 16% of the time, Pallas kernels for 0%

profile of v2, /device:TPU:0, one launch (start us, length us, event | category | flops | bytes accessed | tf_op | source)
XLA Modules:
  0.0 301.5 jit_solution(9084643027880499072)
XLA Ops:
  1.2 3.8 %sort.17 = (s32[256]{0:T(256)}, s32[256]{0:T(256)S(1)}) sort(s32[256]{0:T(256)} %bitcast.98, s32[256]{0:T(256)S(1)} %iota.115), dimensions={0}, to_apply=%region_1.0 | sort | flops 2048 | bytes 4096 | tf_op jit(solution)/shard_map/jit(argsort)/sort | solution.py:113
  5.0 5.0 %gather_fusion = s32[768]{0:T(1024)S(1)} fusion(s32[256]{0:T(256)S(1)} %get-tuple-element.6, s32[1024]{0:T(1024)S(1)} %pad_clamp_fusion.1), kind=kCustom, calls=%fused_computation | custom fusion | bytes 9216 | tf_op jit(solution)/shard_map/gather | solution.py:116
  10.2 5.0 %gather_fusion.1 = s32[768]{0:T(1024)S(1)} fusion(s32[256]{0:T(256)S(1)} %bitcast.82, s32[1024]{0:T(1024)S(1)} %pad_clamp_fusion), kind=kCustom, calls=%fused_computation.1 | custom fusion | bytes 9216 | tf_op jit(solution)/shard_map/gather | solution.py:119
  16.0 7.3 %all-to-all-start = ((s32[8,1,96]{2,1,0:T(1,128)}), s32[8,1,96]{2,1,0:T(1,128)S(1)}, u32[]{:S(2)}, u32[]{:S(2)}) async-start(s32[8,1,96]{2,1,0:T(1,128)} %compare_select_fusion), calls=%async_computation | async-start | bytes 8192 | tf_op jit(solution)/shard_map/all_to_all | solution.py:121
  23.3 1.4 slice_bitcast_fusion.1
  24.7 1.0 fusion.66
  29.2 1.7 fusion.39
  31.3 1.6 subtract_convert_fusion.2
  32.9 2.9 fusion.19
  35.8 2.3 gather_fusion.2
  38.8 1.7 fusion.37
  40.5 1.6 fusion.47
  42.1 2.0 broadcast_select_fusion
  44.1 4.0 %maximum_bitcast_fusion = bf16[1024,2,1024]{0,2,1:T(8,128)(2,1)} fusion(bf16[1,1024,1024]{2,1,0:T(8,128)(2,1)} %bitcast.90, bf16[1,1024,1024]{2,1,0:T(8,128)(2,1)S(1)} %bitcast.89), kind=kLoop, calls=%fused_computation.21 | loop fusion | flops 2097152 | bytes 8388608 | tf_op jit(solution)/shard_map/iul,ruij->lrj/dot_general | solution.py:179
  49.5 1.1 pad_maximum_fusion.v_ref
  51.4 1.3 reshape.846.u_ref
  53.2 1.8 tile.35
  55.4 1.9 tile.39
  58.9 6.3 %copy.54 = bf16[1024,2,1024]{2,0,1:T(8,128)(2,1)} copy(bf16[1024,2,1024]{0,2,1:T(8,128)(2,1)} %maximum_bitcast_fusion) | data formatting | bytes 8388608 | tf_op jit(solution)/shard_map/iul,ruij->lrj/dot_general | solution.py:179
  65.2 6.0 %all-to-all-start.1 = ((f32[8,96,128]{2,1,0:T(8,128)}), f32[8,96,128]{2,1,0:T(8,128)S(1)}, u32[]{:S(2)}, u32[]{:S(2)}) async-start(f32[8,96,128]{2,1,0:T(8,128)} %broadcast_select_fusion), calls=%async_computation.1 | async-start | bytes 786432 | tf_op jit(solution)/shard_map/all_to_all | solution.py:120
  73.4 4.6 %multiply_convert_fusion.4 = bf16[8,16,16,768,2]{3,2,4,1,0:T(8,128)(2,1)} fusion(f32[8,768,2]{1,2,0:T(2,128)S(1)} %copy.55, f32[16,16,768]{2,1,0:T(8,128)S(1)} %and_convert_fusion), kind=kLoop, calls=%fused_computation.8.clone.clone.1 | loop fusion | flops 6291456 | bytes 7127040 | tf_op jit(solution)/shard_map/raqsk,skn->raqn/dot_general | solution.py:150
  78.0 4.4 %all-to-all-done.1 = f32[8,96,128]{2,1,0:T(8,128)S(1)} async-done(((f32[8,96,128]{2,1,0:T(8,128)}), f32[8,96,128]{2,1,0:T(8,128)S(1)}, u32[]{:S(2)}, u32[]{:S(2)}) %all-to-all-start.1) | async-done | bytes 393248 | tf_op jit(solution)/shard_map/all_to_all | solution.py:120
  82.3 0.9 copy.56
  83.3 20.0 %shard_map.55 = bf16[768,2,64,128]{3,2,1,0:T(8,128)(2,1)} custom-call(s32[768]{0:T(1024)} %get-tuple-element.22.plane_ref, f32[128,768]{1,0:T(8,128)} %bitcast.95, bf16[32,64,128]{2,1,0:T(8,128)(2,1)} %reshape.846.u_ref, bf16[32,2,64,128]{3,2,1,0:T(8,128)(2,1)} %pad_maximum_fusion.v_ref), custom_call_target="tpu_custom_call" | custom-call | flops 3221225472 | bytes 50331648 | tf_op jit(solution)/shard_map/pallas_call | solution.py:79
  103.3 34.8 %reshape.847 = bf16[768,2,8192]{2,1,0:T(2,128)(2,1)} reshape(bf16[768,2,64,128]{3,2,1,0:T(8,128)(2,1)} %shard_map.55) | data formatting | bytes 50331648 | tf_op jit(solution)/shard_map/reshape | solution.py:135
  138.0 61.3 %bitcast_convert_fusion = bf16[8,16,16,8192]{3,2,1,0:T(8,128)(2,1)} fusion(bf16[768,2,8192,1,1]{2,1,0,4,3:T(2,128)(2,1)} %bitcast.85, bf16[8,16,16,768,2]{3,2,4,1,0:T(8,128)(2,1)} %multiply_convert_fusion.4), kind=kOutput, calls=%fused_computation.3 | convolution fusion | flops 51556384768 | bytes 65011712 | tf_op jit(solution)/shard_map/raqsk,skn->raqn/dot_general | solution.py:150
  199.3 23.2 %copy.79 = bf16[256,8,64,128]{3,2,1,0:T(8,128)(2,1)} copy(bf16[256,8,64,128]{3,1,2,0:T(8,128)(2,1)} %bitcast.84) | data formatting | bytes 67108864
  222.6 16.4 %bitcast_convert_fusion.1 = bf16[8,16,64,256]{3,2,1,0:T(8,128)(2,1)} fusion(bf16[8,16,16,64,128]{4,3,2,1,0:T(8,128)(2,1)} %bitcast.83, f32[8,128,256]{2,1,0:T(8,128)S(1)} %copy-done.8, f32[8,16,256]{2,1,0:T(8,128)S(1)} %copy-done.12, f32[8,128,256]{2,1,0:T(8,128)S(1)} %copy-done.7, f32[8,16,256]{2,1,0:T(8,128)S(1)} %copy-done.11, ...), kind=kOutput, calls=%fused_computation.12 | convolution fusion | flops 8638169088 | bytes 40173568 | tf_op jit(solution)/shard_map/raqxk,rqkn->raxn/dot_general | solution.py:167
  239.0 6.9 %reshape.849 = bf16[8,1024,2,128]{3,2,1,0:T(2,128)(2,1)} reshape(bf16[8,16,64,256]{3,2,1,0:T(8,128)(2,1)} %bitcast_convert_fusion.1) | data formatting | bytes 8388608 | tf_op jit(solution)/shard_map/reshape | solution.py:168
  245.9 8.0 %bitcast_convert_fusion.2 = bf16[4,256,8,128]{3,1,2,0:T(8,128)(2,1)S(1)} fusion(bf16[8,1024,2,128]{3,2,1,0:T(2,128)(2,1)} %reshape.849, bf16[4,256,2,1024,1]{3,1,0,2,4:T(8,128)(2,1)} %bitcast.91), kind=kOutput, calls=%fused_computation.22 | convolution fusion | flops 4296015872 | bytes 10485760 | tf_op jit(solution)/shard_map/iul,ruij->lrj/dot_general | solution.py:179
  253.9 28.4 %all_to_all.21 = bf16[4,256,8,128]{3,1,2,0:T(8,128)(2,1)S(1)} all-to-all(bf16[4,256,8,128]{3,1,2,0:T(8,128)(2,1)S(1)} %bitcast_convert_fusion.2), channel_id=1, replica_groups=mesh['tile'=8,'chan'=4] {'chan'}, dimensions={0} | all-to-all | bytes 4194304 | tf_op jit(solution)/shard_map/all_to_all | solution.py:182
  283.0 17.6 %all_to_all.22 = bf16[8,256,8,16]{1,3,2,0:T(8,128)(2,1)S(1)} all-to-all(bf16[8,256,8,16]{1,3,2,0:T(8,128)(2,1)S(1)} %copy.64), channel_id=1, replica_groups=mesh['tile'=8,'chan'=4] {'tile'}, dimensions={0} | all-to-all | bytes 1048576 | tf_op jit(solution)/shard_map/all_to_all | solution.py:186
  (95 shorter events, 14.9 us)
Async XLA Ops:
  0.0 35.8 %copy-start = (f32[1,256,128]{2,1,0:T(8,128)S(1)}, f32[1,256,128]{2,1,0:T(8,128)}, u32[]{:S(2)}) copy-start(f32[1,256,128]{2,1,0:T(8,128)} %param.5) | copy-start | bytes 393220
  0.0 10.2 %copy-start.16 = (s32[1,256]{1,0:T(1,128)S(1)}, s32[1,256]{1,0:T(1,128)}, u32[]{:S(2)}) copy-start(s32[1,256]{1,0:T(1,128)} %param.8) | copy-start | bytes 3076
  0.0 10.2 %copy-start.15 = (s32[1,256]{1,0:T(1,128)S(1)}, s32[1,256]{1,0:T(1,128)}, u32[]{:S(2)}) copy-start(s32[1,256]{1,0:T(1,128)} %param.9) | copy-start | bytes 3076
  5.0 18.2 %copy-start.6 = (bf16[1,32,2,64,128]{4,3,2,1,0:T(8,128)(2,1)S(1)}, bf16[1,32,2,64,128]{4,3,2,1,0:T(8,128)(2,1)}, u32[]{:S(2)}) copy-start(bf16[1,32,2,64,128]{4,3,2,1,0:T(8,128)(2,1)} %param.6) | copy-start | bytes 3145732
  16.0 49.3 %all-to-all-start = ((s32[8,1,96]{2,1,0:T(1,128)}), s32[8,1,96]{2,1,0:T(1,128)S(1)}, u32[]{:S(2)}, u32[]{:S(2)}) async-start(s32[8,1,96]{2,1,0:T(1,128)} %compare_select_fusion), calls=%async_computation | async-start | bytes 8192 | tf_op jit(solution)/shard_map/all_to_all | solution.py:121
  44.1 4.1 %copy-start.2 = (bf16[32,64,64]{2,1,0:T(8,128)(2,1)S(1)}, bf16[32,64,64]{2,1,0:T(8,128)(2,1)}, u32[]{:S(2)}) copy-start(bf16[32,64,64]{2,1,0:T(8,128)(2,1)} %fusion.66) | copy-start | bytes 786436
  44.1 4.1 %copy-start.3 = (bf16[32,64,64]{2,1,0:T(8,128)(2,1)S(1)}, bf16[32,64,64]{2,1,0:T(8,128)(2,1)}, u32[]{:S(2)}) copy-start(bf16[32,64,64]{2,1,0:T(8,128)(2,1)} %get-tuple-element.7) | copy-start | bytes 786436
  44.1 4.1 %copy-start.4 = (bf16[32,64,64]{2,1,0:T(8,128)(2,1)S(1)}, bf16[32,64,64]{2,1,0:T(8,128)(2,1)}, u32[]{:S(2)}) copy-start(bf16[32,64,64]{2,1,0:T(8,128)(2,1)} %get-tuple-element.8) | copy-start | bytes 786436
  44.1 4.7 %copy-start.17 = (s32[128]{0:T(128)S(1)}, s32[128]{0:T(128)}, u32[]{:S(2)}) copy-start(s32[128]{0:T(128)} %get-tuple-element.31) | copy-start | bytes 1540
  44.1 4.7 %copy-start.18 = (s32[128]{0:T(128)S(1)}, s32[128]{0:T(128)}, u32[]{:S(2)}) copy-start(s32[128]{0:T(128)} %get-tuple-element.32) | copy-start | bytes 1540
  44.1 4.7 %copy-start.19 = (pred[256]{0:T(512)(128)(4,1)S(1)}, pred[256]{0:T(512)(128)(4,1)}, u32[]{:S(2)}) copy-start(pred[256]{0:T(512)(128)(4,1)} %compare_and_fusion) | copy-start | bytes 772
  44.1 4.7 %copy-start.20 = (pred[128]{0:T(512)(128)(4,1)S(1)}, pred[128]{0:T(512)(128)(4,1)}, u32[]{:S(2)}) copy-start(pred[128]{0:T(512)(128)(4,1)} %compare_and_fusion.1) | copy-start | bytes 388
  48.2 4.6 %copy-start.5 = (f32[8,64,128]{2,1,0:T(8,128)S(1)}, f32[8,64,128]{2,1,0:T(8,128)}, u32[]{:S(2)}) copy-start(f32[8,64,128]{2,1,0:T(8,128)} %get-tuple-element.17) | copy-start | bytes 786436
  51.4 5.9 %copy-start.10 = (f32[8,16,128]{2,1,0:T(8,128)S(1)}, f32[8,16,128]{2,1,0:T(8,128)}, u32[]{:S(2)}) copy-start(f32[8,16,128]{2,1,0:T(8,128)} %get-tuple-element.13) | copy-start | bytes 196612
  51.4 6.7 %copy-start.9 = (f32[8,16,128]{2,1,0:T(8,128)S(1)}, f32[8,16,128]{2,1,0:T(8,128)}, u32[]{:S(2)}) copy-start(f32[8,16,128]{2,1,0:T(8,128)} %get-tuple-element.14) | copy-start | bytes 196612
  65.2 17.1 %all-to-all-start.1 = ((f32[8,96,128]{2,1,0:T(8,128)}), f32[8,96,128]{2,1,0:T(8,128)S(1)}, u32[]{:S(2)}, u32[]{:S(2)}) async-start(f32[8,96,128]{2,1,0:T(8,128)} %broadcast_select_fusion), calls=%async_computation.1 | async-start | bytes 786432 | tf_op jit(solution)/shard_map/all_to_all | solution.py:120
  199.3 23.2 %copy-start.7 = (f32[8,128,256]{2,1,0:T(8,128)S(1)}, f32[8,128,256]{2,1,0:T(8,128)}, u32[]{:S(2)}) copy-start(f32[8,128,256]{2,1,0:T(8,128)} %tile.35) | copy-start | bytes 3145732
  199.3 23.2 %copy-start.8 = (f32[8,128,256]{2,1,0:T(8,128)S(1)}, f32[8,128,256]{2,1,0:T(8,128)}, u32[]{:S(2)}) copy-start(f32[8,128,256]{2,1,0:T(8,128)} %tile.39) | copy-start | bytes 3145732
  199.3 23.2 %copy-start.11 = (f32[8,16,256]{2,1,0:T(8,128)S(1)}, f32[8,16,256]{2,1,0:T(8,128)}, u32[]{:S(2)}) copy-start(f32[8,16,256]{2,1,0:T(8,128)} %tile.33) | copy-start | bytes 393220
  199.3 23.3 %copy-start.12 = (f32[8,16,256]{2,1,0:T(8,128)S(1)}, f32[8,16,256]{2,1,0:T(8,128)}, u32[]{:S(2)}) copy-start(f32[8,16,256]{2,1,0:T(8,128)} %tile.37) | copy-start | bytes 393220
  199.3 23.2 %copy-start.13 = (pred[128,256]{1,0:T(8,128)(4,1)S(1)}, pred[128,256]{1,0:T(8,128)(4,1)}, u32[]{:S(2)}) copy-start(pred[128,256]{1,0:T(8,128)(4,1)} %get-tuple-element.25) | copy-start | bytes 98308
  199.3 23.2 %copy-start.14 = (pred[128,256]{1,0:T(8,128)(4,1)S(1)}, pred[128,256]{1,0:T(8,128)(4,1)}, u32[]{:S(2)}) copy-start(pred[128,256]{1,0:T(8,128)(4,1)} %get-tuple-element.26) | copy-start | bytes 98308
  253.9 47.6 %copy-start.1 = (f32[1,256,128]{2,1,0:T(8,128)S(1)}, f32[1,256,128]{2,1,0:T(8,128)}, u32[]{:S(2)}) copy-start(f32[1,256,128]{2,1,0:T(8,128)} %param.5) | copy-start | bytes 393220

commit v3 on v2

--- a/solution.py
+++ b/solution.py
@@ -116,12 +116,14 @@
     src = order[jnp.clip(first[:, None] + slot[None, :], 0, blocks - 1)]
     packed_meta = cell[0] * NW + plane[0]
     send_samples = jnp.where(valid[:, :, None], samples[src], 0.0)
-    send_meta = jnp.where(valid, packed_meta[src], 0)
-    arrived = lax.all_to_all(send_samples, "tile", split_axis=0, concat_axis=0, tiled=True)
-    arrived_meta = lax.all_to_all(send_meta, "tile", split_axis=0, concat_axis=0, tiled=True)
+    send_meta = jnp.where(valid, packed_meta[src], 0).astype(jnp.float32)
+    meta_row = jnp.pad(send_meta, ((0, 0), (0, samples.shape[1] - capacity)))[:, None, :]
+    arrived = lax.all_to_all(
+        jnp.concatenate([send_samples, meta_row], axis=1), "tile", split_axis=0, concat_axis=0, tiled=True
+    )
     slot_total = tile_count * capacity
-    arrived = arrived.reshape(slot_total, samples.shape[1])
-    arrived_meta = arrived_meta.reshape(slot_total)
+    arrived_meta = arrived[:, capacity, :capacity].astype(jnp.int32).reshape(slot_total)
+    arrived = arrived[:, :capacity, :].reshape(slot_total, samples.shape[1])
 
     slab_rows = G // tile_count
     row_cells = slab_rows // S

time: 303 us -> 296 us (0.977)
  local copies, waits for them, and re-layouts: 96.3 us -> 106 us
  other arithmetic: 35.6 us -> 27.4 us
  starting transfers between devices: 13.3 us -> 7.26 us
  waiting for transfers between devices: 4.37 us -> 0.01 us
    all_to_all x2 -> x1, starting transfers between devices: 13.3 us -> 7.26 us  [local(): lax.all_to_all(jnp.concatenate([send_samples, meta_row], axis=1), 'tile',...]
    all_to_all x2 -> x1, waiting for transfers between devices: 4.37 us -> 0.01 us  [local(): lax.all_to_all(jnp.concatenate([send_samples, meta_row], axis=1), 'tile',...]
    transpose x2, local copies, waits for them, and re-layouts: 0.86 us -> 4.69 us  [patches_rotated(): jnp.transpose(kernel_set[:, :, :, :S], (0, 3, 1, 2)).reshape(NW, S, 2 * S)]
    unnamed x44 -> x34, local copies, waits for them, and re-layouts: 23.4 us -> 23.3 us
  transfers between devices with their start and end apart: 2 -> 1, of which waited for: 1 -> 0; matrix products, arithmetic and copies ran while one was open for 16% -> 15% of each run, Pallas kernels for 0% -> 0%
where the time goes in v3:
time: 296 us; the launch traced here: 294 us
  local copies, waits for them, and re-layouts  106 us (36%)
  matrix products  85 us (29%)
  blocking collectives  48.3 us (16%)
  other arithmetic  27.4 us (9%)
  Pallas kernels  20.2 us (7%)
  starting transfers between devices  7.26 us (2%)
    dot_general x1, matrix products, local(): jnp.einsum('raqsk,skn->raqn', l2, p2, preferred_element_type=jnp.float32)  60.6 us
    reshape x1, local copies, waits for them, and re-layouts, local(): patches_rotated(arrived, plane_r, kernel_set)  34.7 us
    all_to_all x1, blocking collectives, local(): lax.all_to_all(partial.astype(jnp.bfloat16), 'chan', split_axis=0, concat...  28.4 us
    unnamed x34, local copies, waits for them, and re-layouts  23.3 us
    pallas_call x1, Pallas kernels, patches_rotated(): pl.pallas_call(patch_kernel, grid_spec=grid_spec, out_shape=jax.ShapeDtyp...  20.2 us
    all_to_all x1, blocking collectives, local(): lax.all_to_all(partial.astype(jnp.bfloat16), 'tile', split_axis=0, concat...  19.9 us
    dot_general x1, matrix products, local(): jnp.einsum('raqxk,rqkn->raxn', folded, w1, preferred_element_type=jnp.flo...  16.4 us
    dot_general x1, matrix products, local(): jnp.einsum('iul,ruij->lrj', e2, transformed, preferred_element_type=jnp.f...  7.95 us
  transfers between devices with their start and end apart: 1, of which 0 were waited for; matrix products, arithmetic and copies ran while one was open for 15% of the time, Pallas kernels for 0%

profile of v3, /device:TPU:0, one launch (start us, length us, event | category | flops | bytes accessed | tf_op | source)
XLA Modules:
  0.0 294.5 jit_solution(2760206001901667109)
XLA Ops:
  1.3 3.8 %sort.17 = (s32[256]{0:T(256)}, s32[256]{0:T(256)S(1)}) sort(s32[256]{0:T(256)} %bitcast.102, s32[256]{0:T(256)S(1)} %iota.113), dimensions={0}, to_apply=%region_1.0 | sort | flops 2048 | bytes 4096 | tf_op jit(solution)/shard_map/jit(argsort)/sort | solution.py:113
  5.1 5.0 %gather_fusion = s32[768]{0:T(1024)S(1)} fusion(s32[256]{0:T(256)S(1)} %get-tuple-element.6, s32[1024]{0:T(1024)S(1)} %pad_clamp_fusion.1), kind=kCustom, calls=%fused_computation | custom fusion | bytes 9216 | tf_op jit(solution)/shard_map/gather | solution.py:116
  10.3 1.6 gather_fusion.1
  11.9 5.0 %gather_fusion.2 = s32[768]{0:T(1024)S(1)} fusion(s32[256]{0:T(256)S(1)} %bitcast.85, s32[1024]{0:T(1024)S(1)} %pad_clamp_fusion), kind=kCustom, calls=%fused_computation.2 | custom fusion | bytes 9216 | tf_op jit(solution)/shard_map/gather | solution.py:119
  18.0 7.3 %all-to-all-start = ((f32[8,97,128]{2,1,0:T(8,128)}), f32[8,97,128]{2,1,0:T(8,128)}, u32[]{:S(2)}, u32[]{:S(2)}) async-start(f32[8,97,128]{2,1,0:T(8,128)} %pad_maximum_fusion.1), calls=%async_computation | async-start | bytes 851968 | tf_op jit(solution)/shard_map/all_to_all | solution.py:121
  25.4 1.4 slice_bitcast_fusion.1
  26.8 1.0 slice_bitcast_fusion
  30.0 1.7 fusion.39
  32.0 1.6 subtract_convert_fusion.2
  33.6 2.9 fusion.19
  36.6 3.7 %copy.64 = bf16[32,64,2,64]{3,2,1,0:T(2,128)(2,1)} copy(bf16[32,64,2,64]{1,3,0,2:T(8,128)(2,1)} %slice_bitcast_fusion) | data formatting | bytes 1048576 | tf_op jit(solution)/shard_map/transpose | solution.py:63
  40.2 3.1 %reshape.787.u_ref = bf16[32,64,128]{2,1,0:T(8,128)(2,1)} reshape(bf16[32,64,2,64]{3,2,1,0:T(2,128)(2,1)} %copy.64) | data formatting | bytes 1048576 | tf_op jit(solution)/shard_map/reshape | solution.py:63
  44.0 1.0 fusion.37
  45.0 1.4 tile.34
  46.4 3.1 %tile.35 = f32[8,128,256]{2,1,0:T(8,128)} reshape(f32[8,2,64,2,128]{4,3,2,1,0:T(2,128)} %tile.34) | data formatting | bytes 2097152 | tf_op jit(solution)/shard_map/tile | solution.py:162
  49.5 1.4 tile.38
  50.9 3.0 %tile.39 = f32[8,128,256]{2,1,0:T(8,128)} reshape(f32[8,2,64,2,128]{4,3,2,1,0:T(2,128)} %tile.38) | data formatting | bytes 2097152 | tf_op jit(solution)/shard_map/tile | solution.py:163
  55.9 3.9 %maximum_bitcast_fusion = bf16[1024,2,1024]{0,2,1:T(8,128)(2,1)} fusion(bf16[1,1024,1024]{2,1,0:T(8,128)(2,1)} %bitcast.93, bf16[1,1024,1024]{2,1,0:T(8,128)(2,1)S(1)} %bitcast.92), kind=kLoop, calls=%fused_computation.21 | loop fusion | flops 2097152 | bytes 8388608 | tf_op jit(solution)/shard_map/iul,ruij->lrj/dot_general | solution.py:181
  59.8 6.4 %copy.59 = bf16[1024,2,1024]{2,0,1:T(8,128)(2,1)} copy(bf16[1024,2,1024]{0,2,1:T(8,128)(2,1)} %maximum_bitcast_fusion) | data formatting | bytes 8388608 | tf_op jit(solution)/shard_map/iul,ruij->lrj/dot_general | solution.py:181
  67.0 1.1 pad_maximum_fusion.v_ref
  70.5 1.0 slice.27
  71.5 0.9 copy.62
  72.4 20.2 %shard_map.55 = bf16[768,2,64,128]{3,2,1,0:T(8,128)(2,1)} custom-call(s32[768]{0:T(1024)} %get-tuple-element.22.plane_ref, f32[128,768]{1,0:T(8,128)} %bitcast.98, bf16[32,64,128]{2,1,0:T(8,128)(2,1)} %reshape.787.u_ref, bf16[32,2,64,128]{3,2,1,0:T(8,128)(2,1)} %pad_maximum_fusion.v_ref), custom_call_target="tpu_custom_call" | custom-call | flops 3221225472 | bytes 50331648 | tf_op jit(solution)/shard_map/pallas_call | solution.py:79
  92.6 34.7 %reshape.788 = bf16[768,2,8192]{2,1,0:T(2,128)(2,1)} reshape(bf16[768,2,64,128]{3,2,1,0:T(8,128)(2,1)} %shard_map.55) | data formatting | bytes 50331648 | tf_op jit(solution)/shard_map/reshape | solution.py:137
  127.5 1.9 multiply_convert_fusion.4
  129.4 60.6 %bitcast_convert_fusion = bf16[8,16,16,8192]{3,2,1,0:T(8,128)(2,1)} fusion(bf16[768,2,8192,1,1]{2,1,0,4,3:T(2,128)(2,1)} %bitcast.88, bf16[8,16,16,768,2]{3,2,4,1,0:T(8,128)(2,1)S(1)} %multiply_convert_fusion.4), kind=kOutput, calls=%fused_computation.3 | convolution fusion | flops 51556384768 | bytes 65011712 | tf_op jit(solution)/shard_map/raqsk,skn->raqn/dot_general | solution.py:152
  190.0 23.2 %copy.85 = bf16[256,8,64,128]{3,2,1,0:T(8,128)(2,1)} copy(bf16[256,8,64,128]{3,1,2,0:T(8,128)(2,1)} %bitcast.87) | data formatting | bytes 67108864
  213.3 16.4 %bitcast_convert_fusion.1 = bf16[8,16,64,256]{3,2,1,0:T(8,128)(2,1)} fusion(bf16[8,16,16,64,128]{4,3,2,1,0:T(8,128)(2,1)} %bitcast.86, f32[8,128,256]{2,1,0:T(8,128)S(1)} %copy-done.6, f32[8,16,256]{2,1,0:T(8,128)S(1)} %copy-done.8, f32[8,128,256]{2,1,0:T(8,128)S(1)} %copy-done.5, f32[8,16,256]{2,1,0:T(8,128)S(1)} %copy-done.7, ...), kind=kOutput, calls=%fused_computation.12 | convolution fusion | flops 8638169088 | bytes 40173568 | tf_op jit(solution)/shard_map/raqxk,rqkn->raxn/dot_general | solution.py:169
  229.7 6.9 %reshape.790 = bf16[8,1024,2,128]{3,2,1,0:T(2,128)(2,1)} reshape(bf16[8,16,64,256]{3,2,1,0:T(8,128)(2,1)} %bitcast_convert_fusion.1) | data formatting | bytes 8388608 | tf_op jit(solution)/shard_map/reshape | solution.py:170
  236.6 7.9 %bitcast_convert_fusion.2 = bf16[4,256,8,128]{3,1,2,0:T(8,128)(2,1)S(1)} fusion(bf16[8,1024,2,128]{3,2,1,0:T(2,128)(2,1)} %reshape.790, bf16[4,256,2,1024,1]{3,1,0,2,4:T(8,128)(2,1)} %bitcast.94), kind=kOutput, calls=%fused_computation.22 | convolution fusion | flops 4296015872 | bytes 10485760 | tf_op jit(solution)/shard_map/iul,ruij->lrj/dot_general | solution.py:181
  244.6 28.4 %all_to_all.15 = bf16[4,256,8,128]{3,1,2,0:T(8,128)(2,1)S(1)} all-to-all(bf16[4,256,8,128]{3,1,2,0:T(8,128)(2,1)S(1)} %bitcast_convert_fusion.2), channel_id=1, replica_groups=mesh['tile'=8,'chan'=4] {'chan'}, dimensions={0} | all-to-all | bytes 4194304 | tf_op jit(solution)/shard_map/all_to_all | solution.py:184
  273.6 19.9 %all_to_all.16 = bf16[8,256,8,16]{1,3,2,0:T(8,128)(2,1)S(1)} all-to-all(bf16[8,256,8,16]{1,3,2,0:T(8,128)(2,1)S(1)} %copy.70), channel_id=1, replica_groups=mesh['tile'=8,'chan'=4] {'tile'}, dimensions={0} | all-to-all | bytes 1048576 | tf_op jit(solution)/shard_map/all_to_all | solution.py:188
  (85 shorter events, 12.6 us)
Async XLA Ops:
  0.0 10.3 %copy-start = (f32[1,256,128]{2,1,0:T(8,128)S(1)}, f32[1,256,128]{2,1,0:T(8,128)}, u32[]{:S(2)}) copy-start(f32[1,256,128]{2,1,0:T(8,128)} %param.5) | copy-start | bytes 393220
  0.0 11.8 %copy-start.12 = (s32[1,256]{1,0:T(1,128)S(1)}, s32[1,256]{1,0:T(1,128)}, u32[]{:S(2)}) copy-start(s32[1,256]{1,0:T(1,128)} %param.8) | copy-start | bytes 3076
  0.0 11.9 %copy-start.11 = (s32[1,256]{1,0:T(1,128)S(1)}, s32[1,256]{1,0:T(1,128)}, u32[]{:S(2)}) copy-start(s32[1,256]{1,0:T(1,128)} %param.9) | copy-start | bytes 3076
  11.9 13.4 %copy-start.4 = (bf16[1,32,2,64,128]{4,3,2,1,0:T(8,128)(2,1)S(1)}, bf16[1,32,2,64,128]{4,3,2,1,0:T(8,128)(2,1)}, u32[]{:S(2)}) copy-start(bf16[1,32,2,64,128]{4,3,2,1,0:T(8,128)(2,1)} %param.6) | copy-start | bytes 3145732
  18.0 50.9 %all-to-all-start = ((f32[8,97,128]{2,1,0:T(8,128)}), f32[8,97,128]{2,1,0:T(8,128)}, u32[]{:S(2)}, u32[]{:S(2)}) async-start(f32[8,97,128]{2,1,0:T(8,128)} %pad_maximum_fusion.1), calls=%async_computation | async-start | bytes 851968 | tf_op jit(solution)/shard_map/all_to_all | solution.py:121
  40.2 13.7 %copy-start.15 = (s32[16]{0:T(128)S(1)}, s32[16]{0:T(128)}, u32[]{:S(2)}) copy-start(s32[16]{0:T(128)} %iota_multiply_fusion) | copy-start | bytes 196
  59.8 6.6 %copy-start.2 = (bf16[32,64,64]{2,1,0:T(8,128)(2,1)S(1)}, bf16[32,64,64]{2,1,0:T(8,128)(2,1)}, u32[]{:S(2)}) copy-start(bf16[32,64,64]{2,1,0:T(8,128)(2,1)} %get-tuple-element.7) | copy-start | bytes 786436
  59.8 6.6 %copy-start.3 = (bf16[32,64,64]{2,1,0:T(8,128)(2,1)S(1)}, bf16[32,64,64]{2,1,0:T(8,128)(2,1)}, u32[]{:S(2)}) copy-start(bf16[32,64,64]{2,1,0:T(8,128)(2,1)} %get-tuple-element.8) | copy-start | bytes 786436
  66.1 2.0 copy-start.13
  66.1 2.0 copy-start.14
  190.0 23.2 %copy-start.5 = (f32[8,128,256]{2,1,0:T(8,128)S(1)}, f32[8,128,256]{2,1,0:T(8,128)}, u32[]{:S(2)}) copy-start(f32[8,128,256]{2,1,0:T(8,128)} %tile.35) | copy-start | bytes 3145732
  190.0 23.2 %copy-start.6 = (f32[8,128,256]{2,1,0:T(8,128)S(1)}, f32[8,128,256]{2,1,0:T(8,128)}, u32[]{:S(2)}) copy-start(f32[8,128,256]{2,1,0:T(8,128)} %tile.39) | copy-start | bytes 3145732
  190.0 23.2 %copy-start.7 = (f32[8,16,256]{2,1,0:T(8,128)S(1)}, f32[8,16,256]{2,1,0:T(8,128)}, u32[]{:S(2)}) copy-start(f32[8,16,256]{2,1,0:T(8,128)} %tile.33) | copy-start | bytes 393220
  190.0 23.2 %copy-start.8 = (f32[8,16,256]{2,1,0:T(8,128)S(1)}, f32[8,16,256]{2,1,0:T(8,128)}, u32[]{:S(2)}) copy-start(f32[8,16,256]{2,1,0:T(8,128)} %tile.37) | copy-start | bytes 393220
  190.0 23.2 %copy-start.9 = (pred[128,256]{1,0:T(8,128)(4,1)S(1)}, pred[128,256]{1,0:T(8,128)(4,1)}, u32[]{:S(2)}) copy-start(pred[128,256]{1,0:T(8,128)(4,1)} %get-tuple-element.25) | copy-start | bytes 98308
  190.0 23.2 %copy-start.10 = (pred[128,256]{1,0:T(8,128)(4,1)S(1)}, pred[128,256]{1,0:T(8,128)(4,1)}, u32[]{:S(2)}) copy-start(pred[128,256]{1,0:T(8,128)(4,1)} %get-tuple-element.26) | copy-start | bytes 98308
  244.6 49.9 %copy-start.1 = (f32[1,256,128]{2,1,0:T(8,128)S(1)}, f32[1,256,128]{2,1,0:T(8,128)}, u32[]{:S(2)}) copy-start(f32[1,256,128]{2,1,0:T(8,128)} %param.5) | copy-start | bytes 393220

commit v4 on v3

--- a/solution.py
+++ b/solution.py
@@ -180,12 +180,12 @@
     e2 = jnp.stack([c2, -s2])
     partial = jnp.einsum("iul,ruij->lrj", e2, transformed, preferred_element_type=jnp.float32)
     chan_count = lax.axis_size("chan")
-    partial = partial.reshape(chan_count, P_SIZE // chan_count, NF, j_len)
-    partial = lax.all_to_all(partial.astype(jnp.bfloat16), "chan", split_axis=0, concat_axis=0, tiled=True)
-    partial = jnp.sum(partial.astype(jnp.float32), axis=0)
-    partial = partial.reshape(P_SIZE // chan_count, NF, tile_count, j_len // tile_count)
+    partial = partial.reshape(P_SIZE, NF, tile_count, j_len // tile_count)
     partial = jnp.transpose(partial, (2, 0, 1, 3))
     partial = lax.all_to_all(partial.astype(jnp.bfloat16), "tile", split_axis=0, concat_axis=0, tiled=True)
+    partial = jnp.sum(partial.astype(jnp.float32), axis=0)
+    partial = partial.reshape(chan_count, P_SIZE // chan_count, NF, j_len // tile_count)
+    partial = lax.all_to_all(partial.astype(jnp.bfloat16), "chan", split_axis=0, concat_axis=0, tiled=True)
     partial = jnp.sum(partial.astype(jnp.float32), axis=0)
     out = jnp.transpose(partial, (0, 2, 1))
     return out.reshape(out.shape[0], -1) * (1.0 / G)

time: 296 us -> 296 us (level)
  blocking collectives: 48.3 us -> 62.2 us
  other arithmetic: 27.4 us -> 19.5 us
  local copies, waits for them, and re-layouts: 106 us -> 101 us
    all_to_all x1, blocking collectives: 19.9 us -> 53.6 us  [local(): lax.all_to_all(partial.astype(jnp.bfloat16), 'tile', split_axis=0, concat...]
    all_to_all x1, blocking collectives: 28.4 us -> 8.63 us  [local(): lax.all_to_all(partial.astype(jnp.bfloat16), 'chan', split_axis=0, concat...]
    reshape x1 -> x2, local copies, waits for them, and re-layouts: 6.89 us -> 18.3 us  [local(): transformed.astype(jnp.bfloat16).reshape(NF, slab_rows, 2, j_len)]
    dot_general x1 -> x0, local copies, waits for them, and re-layouts: 6.37 us -> none  [local(): jnp.einsum('iul,ruij->lrj', e2, transformed, preferred_element_type=jnp.f...]
    dot_general x1 -> x0, other arithmetic: 3.91 us -> none  [local(): jnp.einsum('iul,ruij->lrj', e2, transformed, preferred_element_type=jnp.f...]
    transpose x2, local copies, waits for them, and re-layouts: 4.69 us -> 0.87 us  [patches_rotated(): jnp.transpose(kernel_set[:, :, :, :S], (0, 3, 1, 2)).reshape(NW, S, 2 * S)]
    unnamed x34 -> x28, local copies, waits for them, and re-layouts: 23.3 us -> 23.3 us
  transfers between devices with their start and end apart: 1 -> 1, of which waited for: 0 -> 0; matrix products, arithmetic and copies ran while one was open for 15% -> 6% of each run, Pallas kernels for 0% -> 0%
where the time goes in v4:
time: 296 us; the launch traced here: 295 us
  local copies, waits for them, and re-layouts  101 us (34%)
  matrix products  84.4 us (29%)
  blocking collectives  62.2 us (21%)
  Pallas kernels  20.2 us (7%)
  other arithmetic  19.5 us (7%)
  starting transfers between devices  7.26 us (2%)
    dot_general x1, matrix products, local(): jnp.einsum('raqsk,skn->raqn', l2, p2, preferred_element_type=jnp.float32)  60.6 us
    all_to_all x1, blocking collectives, local(): lax.all_to_all(partial.astype(jnp.bfloat16), 'tile', split_axis=0, concat...  53.6 us
    reshape x1, local copies, waits for them, and re-layouts, local(): patches_rotated(arrived, plane_r, kernel_set)  34.8 us
    unnamed x28, local copies, waits for them, and re-layouts  23.3 us
    pallas_call x1, Pallas kernels, patches_rotated(): pl.pallas_call(patch_kernel, grid_spec=grid_spec, out_shape=jax.ShapeDtyp...  20.2 us
    reshape x2, local copies, waits for them, and re-layouts, local(): transformed.astype(jnp.bfloat16).reshape(NF, slab_rows, 2, j_len)  18.3 us
    dot_general x1, matrix products, local(): jnp.einsum('raqxk,rqkn->raxn', folded, w1, preferred_element_type=jnp.flo...  16.4 us
    all_to_all x1, blocking collectives, local(): lax.all_to_all(partial.astype(jnp.bfloat16), 'chan', split_axis=0, concat...  8.63 us
  transfers between devices with their start and end apart: 1, of which 0 were waited for; matrix products, arithmetic and copies ran while one was open for 6% of the time, Pallas kernels for 0%

profile of v4, /device:TPU:0, one launch (start us, length us, event | category | flops | bytes accessed | tf_op | source)
XLA Modules:
  0.0 294.7 jit_solution(2677822386212240466)
XLA Ops:
  0.0 0.8 convert_reduce_fusion.1
  1.3 3.8 %sort.17 = (s32[256]{0:T(256)}, s32[256]{0:T(256)S(1)}) sort(s32[256]{0:T(256)} %bitcast.113, s32[256]{0:T(256)S(1)} %iota.113), dimensions={0}, to_apply=%region_1.0 | sort | flops 2048 | bytes 4096 | tf_op jit(solution)/shard_map/jit(argsort)/sort | solution.py:113
  5.1 5.0 %gather_fusion = s32[768]{0:T(1024)S(1)} fusion(s32[256]{0:T(256)S(1)} %get-tuple-element.6, s32[1024]{0:T(1024)S(1)} %pad_clamp_fusion.1), kind=kCustom, calls=%fused_computation | custom fusion | bytes 9216 | tf_op jit(solution)/shard_map/gather | solution.py:116
  10.3 1.6 gather_fusion.1
  11.9 5.0 %gather_fusion.2 = s32[768]{0:T(1024)S(1)} fusion(s32[256]{0:T(256)S(1)} %bitcast.95, s32[1024]{0:T(1024)S(1)} %pad_clamp_fusion), kind=kCustom, calls=%fused_computation.2 | custom fusion | bytes 9216 | tf_op jit(solution)/shard_map/gather | solution.py:119
  17.2 0.8 pad_maximum_fusion.1
  18.0 7.3 %all-to-all-start = ((f32[8,97,128]{2,1,0:T(8,128)}), f32[8,97,128]{2,1,0:T(8,128)}, u32[]{:S(2)}, u32[]{:S(2)}) async-start(f32[8,97,128]{2,1,0:T(8,128)} %pad_maximum_fusion.1), calls=%async_computation | async-start | bytes 851968 | tf_op jit(solution)/shard_map/all_to_all | solution.py:121
  25.4 1.2 slice_bitcast_fusion.1
  26.9 0.8 copy.62
  27.7 1.3 reshape.787.u_ref
  29.0 1.0 fusion.37
  30.5 1.8 tile.35
  32.7 1.9 tile.39
  35.8 0.8 tile.37
  36.5 1.0 fusion.39
  39.3 1.1 pad_maximum_fusion.v_ref
  40.4 2.0 subtract_convert_fusion.2
  42.4 2.0 fusion.20
  44.4 0.8 fusion.60
  46.0 1.0 slice.27
  47.0 0.9 copy.60
  48.0 20.2 %shard_map.55 = bf16[768,2,64,128]{3,2,1,0:T(8,128)(2,1)} custom-call(s32[768]{0:T(1024)} %get-tuple-element.22.plane_ref, f32[128,768]{1,0:T(8,128)} %bitcast.107, bf16[32,64,128]{2,1,0:T(8,128)(2,1)} %reshape.787.u_ref, bf16[32,2,64,128]{3,2,1,0:T(8,128)(2,1)} %pad_maximum_fusion.v_ref), custom_call_target="tpu_custom_call" | custom-call | flops 3221225472 | bytes 50331648 | tf_op jit(solution)/shard_map/pallas_call | solution.py:79
  68.1 34.8 %reshape.788 = bf16[768,2,8192]{2,1,0:T(2,128)(2,1)} reshape(bf16[768,2,64,128]{3,2,1,0:T(8,128)(2,1)} %shard_map.55) | data formatting | bytes 50331648 | tf_op jit(solution)/shard_map/reshape | solution.py:137
  103.0 1.9 multiply_convert_fusion.4
  105.0 60.6 %bitcast_convert_fusion = bf16[8,16,16,8192]{3,2,1,0:T(8,128)(2,1)} fusion(bf16[768,2,8192,1,1]{2,1,0,4,3:T(2,128)(2,1)} %bitcast.98, bf16[8,16,16,768,2]{3,2,4,1,0:T(8,128)(2,1)S(1)} %multiply_convert_fusion.4), kind=kOutput, calls=%fused_computation.3 | convolution fusion | flops 51556384768 | bytes 65011712 | tf_op jit(solution)/shard_map/raqsk,skn->raqn/dot_general | solution.py:152
  165.6 23.2 %copy.82 = bf16[256,8,64,128]{3,2,1,0:T(8,128)(2,1)} copy(bf16[256,8,64,128]{3,1,2,0:T(8,128)(2,1)} %bitcast.97) | data formatting | bytes 67108864
  188.9 16.4 %bitcast_convert_fusion.1 = bf16[8,16,64,256]{3,2,1,0:T(8,128)(2,1)} fusion(bf16[8,16,16,64,128]{4,3,2,1,0:T(8,128)(2,1)} %bitcast.96, f32[8,128,256]{2,1,0:T(8,128)S(1)} %copy-done.6, f32[8,16,256]{2,1,0:T(8,128)S(1)} %copy-done.8, f32[8,128,256]{2,1,0:T(8,128)S(1)} %copy-done.5, f32[8,16,256]{2,1,0:T(8,128)S(1)} %copy-done.7, ...), kind=kOutput, calls=%fused_computation.12 | convolution fusion | flops 8638169088 | bytes 40173568 | tf_op jit(solution)/shard_map/raqxk,rqkn->raxn/dot_general | solution.py:169
  205.3 6.9 %reshape.790 = bf16[8,1024,2,128]{3,2,1,0:T(2,128)(2,1)} reshape(bf16[8,16,64,256]{3,2,1,0:T(8,128)(2,1)} %bitcast_convert_fusion.1) | data formatting | bytes 8388608 | tf_op jit(solution)/shard_map/reshape | solution.py:170
  212.2 11.3 %copy.65 = bf16[8,1024,2,128]{1,3,2,0:T(8,128)(2,1)} copy(bf16[8,1024,2,128]{3,2,1,0:T(2,128)(2,1)} %reshape.790) | data formatting | bytes 8388608 | tf_op jit(solution)/shard_map/reshape | solution.py:170
  223.6 7.4 %fusion.21 = bf16[8,1024,8,16]{1,3,0,2:T(8,128)(2,1)S(1)} fusion(bf16[8,8,16,2,1024]{4,2,1,3,0:T(8,128)(2,1)} %bitcast.102, bf16[1,1024,1024]{2,1,0:T(8,128)(2,1)} %bitcast.104, bf16[1,1024,1024]{2,1,0:T(8,128)(2,1)S(1)} %bitcast.103), kind=kOutput, calls=%fused_computation.30 | convolution fusion | flops 4304404480 | bytes 10485760 | tf_op jit(solution)/shard_map/iul,ruij->lrj/dot_general | solution.py:181
  231.2 53.6 %all_to_all.15 = bf16[8,1024,8,16]{1,3,2,0:T(8,128)(2,1)S(1)} all-to-all(bf16[8,1024,8,16]{1,3,2,0:T(8,128)(2,1)S(1)} %copy.67), channel_id=1, replica_groups=mesh['tile'=8,'chan'=4] {'tile'}, dimensions={0} | all-to-all | bytes 4194304 | tf_op jit(solution)/shard_map/all_to_all | solution.py:185
  285.2 8.6 %all_to_all.16 = bf16[4,256,8,16]{1,3,2,0:T(8,128)(2,1)S(1)} all-to-all(bf16[4,256,8,16]{1,3,2,0:T(8,128)(2,1)S(1)} %bitcast.109), channel_id=1, replica_groups=mesh['tile'=8,'chan'=4] {'chan'}, dimensions={0} | all-to-all | bytes 524288 | tf_op jit(solution)/shard_map/all_to_all | solution.py:188
  (78 shorter events, 7.5 us)
Async XLA Ops:
  0.0 10.3 %copy-start = (f32[1,256,128]{2,1,0:T(8,128)S(1)}, f32[1,256,128]{2,1,0:T(8,128)}, u32[]{:S(2)}) copy-start(f32[1,256,128]{2,1,0:T(8,128)} %param.5) | copy-start | bytes 393220
  0.0 11.8 %copy-start.12 = (s32[1,256]{1,0:T(1,128)S(1)}, s32[1,256]{1,0:T(1,128)}, u32[]{:S(2)}) copy-start(s32[1,256]{1,0:T(1,128)} %param.8) | copy-start | bytes 3076
  0.0 11.9 %copy-start.11 = (s32[1,256]{1,0:T(1,128)S(1)}, s32[1,256]{1,0:T(1,128)}, u32[]{:S(2)}) copy-start(s32[1,256]{1,0:T(1,128)} %param.9) | copy-start | bytes 3076
  5.1 20.2 %copy-start.4 = (bf16[1,32,2,64,128]{4,3,2,1,0:T(8,128)(2,1)S(1)}, bf16[1,32,2,64,128]{4,3,2,1,0:T(8,128)(2,1)}, u32[]{:S(2)}) copy-start(bf16[1,32,2,64,128]{4,3,2,1,0:T(8,128)(2,1)} %param.6) | copy-start | bytes 3145732
  18.0 26.4 %all-to-all-start = ((f32[8,97,128]{2,1,0:T(8,128)}), f32[8,97,128]{2,1,0:T(8,128)}, u32[]{:S(2)}, u32[]{:S(2)}) async-start(f32[8,97,128]{2,1,0:T(8,128)} %pad_maximum_fusion.1), calls=%async_computation | async-start | bytes 851968 | tf_op jit(solution)/shard_map/all_to_all | solution.py:121
  29.0 8.9 %copy-start.3 = (bf16[32,64,64]{2,1,0:T(8,128)(2,1)S(1)}, bf16[32,64,64]{2,1,0:T(8,128)(2,1)}, u32[]{:S(2)}) copy-start(bf16[32,64,64]{2,1,0:T(8,128)(2,1)} %get-tuple-element.8) | copy-start | bytes 786436
  165.6 23.2 %copy-start.5 = (f32[8,128,256]{2,1,0:T(8,128)S(1)}, f32[8,128,256]{2,1,0:T(8,128)}, u32[]{:S(2)}) copy-start(f32[8,128,256]{2,1,0:T(8,128)} %tile.35) | copy-start | bytes 3145732
  165.6 23.2 %copy-start.6 = (f32[8,128,256]{2,1,0:T(8,128)S(1)}, f32[8,128,256]{2,1,0:T(8,128)}, u32[]{:S(2)}) copy-start(f32[8,128,256]{2,1,0:T(8,128)} %tile.39) | copy-start | bytes 3145732
  165.6 23.2 %copy-start.7 = (f32[8,16,256]{2,1,0:T(8,128)S(1)}, f32[8,16,256]{2,1,0:T(8,128)}, u32[]{:S(2)}) copy-start(f32[8,16,256]{2,1,0:T(8,128)} %tile.33) | copy-start | bytes 393220
  165.6 23.3 %copy-start.8 = (f32[8,16,256]{2,1,0:T(8,128)S(1)}, f32[8,16,256]{2,1,0:T(8,128)}, u32[]{:S(2)}) copy-start(f32[8,16,256]{2,1,0:T(8,128)} %tile.37) | copy-start | bytes 393220
  165.6 23.3 %copy-start.9 = (pred[128,256]{1,0:T(8,128)(4,1)S(1)}, pred[128,256]{1,0:T(8,128)(4,1)}, u32[]{:S(2)}) copy-start(pred[128,256]{1,0:T(8,128)(4,1)} %get-tuple-element.25) | copy-start | bytes 98308
  165.6 23.3 %copy-start.10 = (pred[128,256]{1,0:T(8,128)(4,1)S(1)}, pred[128,256]{1,0:T(8,128)(4,1)}, u32[]{:S(2)}) copy-start(pred[128,256]{1,0:T(8,128)(4,1)} %get-tuple-element.26) | copy-start | bytes 98308
  212.2 11.3 %copy-start.2 = (bf16[16,64,1024]{2,1,0:T(8,128)(2,1)S(1)}, bf16[16,64,1024]{2,1,0:T(8,128)(2,1)}, u32[]{:S(2)}) copy-start(bf16[16,64,1024]{2,1,0:T(8,128)(2,1)} %subtract_convert_fusion.2) | copy-start | bytes 6291460
  223.6 71.1 %copy-start.1 = (f32[1,256,128]{2,1,0:T(8,128)S(1)}, f32[1,256,128]{2,1,0:T(8,128)}, u32[]{:S(2)}) copy-start(f32[1,256,128]{2,1,0:T(8,128)} %param.5) | copy-start | bytes 393220

commit v5 on v3

--- a/solution.py
+++ b/solution.py
@@ -106,17 +106,18 @@
     capacity = 3 * blocks // tile_count
     spacing = G // P_SIZE - 1
 
-    counts = jnp.sum(
-        (owners[:, None] == jnp.arange(tile_count, dtype=jnp.int32)[None, :]).astype(jnp.int32), axis=0
-    )
-    first = jnp.cumsum(counts) - counts
-    order = jnp.argsort(owners, stable=True).astype(jnp.int32)
+    tiles = jnp.arange(tile_count, dtype=jnp.int32)
+    onehot = (owners[:, None] == tiles[None, :]).astype(jnp.int32)
+    rank = jnp.sum(jnp.cumsum(onehot, axis=0) * onehot, axis=1) - 1
     slot = jnp.arange(capacity, dtype=jnp.int32)
-    valid = slot[None, :] < counts[:, None]
-    src = order[jnp.clip(first[:, None] + slot[None, :], 0, blocks - 1)]
-    packed_meta = cell[0] * NW + plane[0]
-    send_samples = jnp.where(valid[:, :, None], samples[src], 0.0)
-    send_meta = jnp.where(valid, packed_meta[src], 0).astype(jnp.float32)
+    pick = (owners[None, None, :] == tiles[:, None, None]) & (rank[None, None, :] == slot[None, :, None])
+    pick = pick.astype(jnp.float32).reshape(tile_count * capacity, blocks)
+    packed_meta = (cell[0] * NW + plane[0]).astype(jnp.float32)
+    routed = jnp.dot(
+        pick, jnp.concatenate([samples, packed_meta[:, None]], axis=1), precision=lax.Precision.HIGHEST
+    )
+    send_samples = routed[:, : samples.shape[1]].reshape(tile_count, capacity, samples.shape[1])
+    send_meta = routed[:, samples.shape[1]].reshape(tile_count, capacity)
     meta_row = jnp.pad(send_meta, ((0, 0), (0, samples.shape[1] - capacity)))[:, None, :]
     arrived = lax.all_to_all(
         jnp.concatenate([send_samples, meta_row], axis=1), "tile", split_axis=0, concat_axis=0, tiled=True
@@ -152,15 +153,17 @@
     folded = jnp.einsum("raqsk,skn->raqn", l2, p2, preferred_element_type=jnp.float32).astype(jnp.bfloat16)
     folded = folded.reshape(NF, row_cells, q_cells, S, 2 * S)
 
-    j_index = resid[:, None] + NF * (jnp.arange(j_len, dtype=jnp.int32)[None, :] - j_len // 2)
     coarse = jnp.arange(q_cells, dtype=jnp.int32) * S
     fine = jnp.arange(S, dtype=jnp.int32)
-    ca, sa = cos_sin_f32(jnp.mod(coarse[None, :, None] * (spacing * j_index[:, None, :]), G))
-    cb, sb = cos_sin_f32(jnp.mod(fine[None, :, None] * (spacing * j_index[:, None, :]), G))
-    ca = jnp.tile(ca, (1, 1, 2))[:, :, None, :]
-    sa = jnp.tile(sa, (1, 1, 2))[:, :, None, :]
-    cb = jnp.tile(cb, (1, 2, 2))[:, None, :, :]
-    sb = jnp.tile(sb, (1, 2, 2))[:, None, :, :]
+    n_full = jnp.arange(2 * j_len, dtype=jnp.int32) % j_len
+    j_full = resid[:, None] + NF * (n_full[None, :] - j_len // 2)
+    y_full = jnp.arange(2 * S, dtype=jnp.int32) % S
+    ca, sa = cos_sin_f32(jnp.mod(coarse[None, :, None] * (spacing * j_full[:, None, :]), G))
+    cb, sb = cos_sin_f32(jnp.mod(y_full[None, :, None] * (spacing * j_full[:, None, :]), G))
+    ca = ca[:, :, None, :]
+    sa = sa[:, :, None, :]
+    cb = cb[:, None, :, :]
+    sb = sb[:, None, :, :]
     c1 = (ca * cb - sa * sb).astype(jnp.bfloat16)
     s1 = (sa * cb + ca * sb).astype(jnp.bfloat16)
     ri_in = lax.broadcasted_iota(jnp.int32, (1, 1, 2 * S, 2 * j_len), 2) // S
@@ -171,14 +174,14 @@
 
     l_index = jnp.arange(P_SIZE, dtype=jnp.int32) - P_SIZE // 2
     row_base = (tile_index * slab_rows - G // 2) + jnp.arange(row_cells, dtype=jnp.int32) * S
-    ca, sa = cos_sin_f32(phase_index(row_base, l_index))
-    cb, sb = cos_sin_f32(phase_index(fine, l_index))
-    c2 = (ca[:, None, :] * cb[None, :, :] - sa[:, None, :] * sb[None, :, :]).astype(jnp.bfloat16)
-    s2 = (sa[:, None, :] * cb[None, :, :] + ca[:, None, :] * sb[None, :, :]).astype(jnp.bfloat16)
-    c2 = c2.reshape(slab_rows, P_SIZE)
-    s2 = s2.reshape(slab_rows, P_SIZE)
-    e2 = jnp.stack([c2, -s2])
-    partial = jnp.einsum("iul,ruij->lrj", e2, transformed, preferred_element_type=jnp.float32)
+    ca, sa = cos_sin_f32(phase_index(l_index, row_base))
+    cb, sb = cos_sin_f32(phase_index(l_index, fine))
+    c2 = (ca[:, :, None] * cb[:, None, :] - sa[:, :, None] * sb[:, None, :]).astype(jnp.bfloat16)
+    s2 = (sa[:, :, None] * cb[:, None, :] + ca[:, :, None] * sb[:, None, :]).astype(jnp.bfloat16)
+    c2 = c2.reshape(P_SIZE, slab_rows)
+    s2 = s2.reshape(P_SIZE, slab_rows)
+    e2 = jnp.stack([c2, -s2], axis=1)
+    partial = jnp.einsum("liu,ruij->lrj", e2, transformed, preferred_element_type=jnp.float32)
     chan_count = lax.axis_size("chan")
     partial = partial.reshape(chan_count, P_SIZE // chan_count, NF, j_len)
     partial = lax.all_to_all(partial.astype(jnp.bfloat16), "chan", split_axis=0, concat_axis=0, tiled=True)

time: 296 us -> 278 us (0.939)
  local copies, waits for them, and re-layouts: 106 us -> 91.4 us
  other arithmetic: 27.4 us -> 23.3 us
    gather x5 -> x0, local copies, waits for them, and re-layouts: 11.7 us -> none  [the longest x2 5.06 us: local(): send_meta = jnp.where(valid, packed_meta[src], 0).astype(jnp.float32)]
    another operation x8 -> x2, local copies, waits for them, and re-layouts: 10.5 us -> 0.08 us  [the longest x1 0.07 us: local(): send_meta = routed[:, samples.shape[1]].reshape(tile_count, capacity)]
    convert_element_type x0 -> x3, local copies, waits for them, and re-layouts: none -> 8.93 us  [the longest x2 8.79 us: local(): (ca[:, :, None] * cb[:, None, :] - sa[:, :, None] * sb[:, None, :]).astyp...]
    neg x0 -> x2, local copies, waits for them, and re-layouts: none -> 7.15 us  [local(): e2 = jnp.stack([c2, -s2], axis=1)]
    dot_general x1 -> x0, local copies, waits for them, and re-layouts: 6.37 us -> none  [local(): jnp.einsum('iul,ruij->lrj', e2, transformed, preferred_element_type=jnp.f...]
    cos x4, other arithmetic: 3.43 us -> 8.64 us  [cos_sin_f32(): return (jnp.cos(angle), jnp.sin(angle))]
    dot_general x1 -> x0, other arithmetic: 3.91 us -> none  [local(): jnp.einsum('iul,ruij->lrj', e2, transformed, preferred_element_type=jnp.f...]
    sort x1 -> x0, other arithmetic: 3.84 us -> none  [local(): order = jnp.argsort(owners, stable=True).astype(jnp.int32)]
  transfers between devices with their start and end apart: 1 -> 1, of which waited for: 0 -> 0; matrix products, arithmetic and copies ran while one was open for 15% -> 14% of each run, Pallas kernels for 0% -> 0%
where the time goes in v5:
time: 278 us; the launch traced here: 276 us
  local copies, waits for them, and re-layouts  91.4 us (33%)
  matrix products  85.6 us (31%)
  blocking collectives  48.2 us (17%)
  other arithmetic  23.3 us (8%)
  Pallas kernels  20 us (7%)
  starting transfers between devices  7.25 us (3%)
    dot_general x1, matrix products, local(): jnp.einsum('raqsk,skn->raqn', l2, p2, preferred_element_type=jnp.float32)  60.7 us
    reshape x1, local copies, waits for them, and re-layouts, local(): patches_rotated(arrived, plane_r, kernel_set)  34.8 us
    all_to_all x1, blocking collectives, local(): lax.all_to_all(partial.astype(jnp.bfloat16), 'chan', split_axis=0, concat...  28.3 us
    unnamed x24, local copies, waits for them, and re-layouts  23.3 us
    pallas_call x1, Pallas kernels, patches_rotated(): pl.pallas_call(patch_kernel, grid_spec=grid_spec, out_shape=jax.ShapeDtyp...  20 us
    all_to_all x1, blocking collectives, local(): lax.all_to_all(partial.astype(jnp.bfloat16), 'tile', split_axis=0, concat...  19.9 us
    dot_general x1, matrix products, local(): jnp.einsum('raqxk,rqkn->raxn', folded, w1, preferred_element_type=jnp.flo...  16.2 us
    convert_element_type x2, local copies, waits for them, and re-layouts, local(): (ca[:, :, None] * cb[:, None, :] - sa[:, :, None] * sb[:, None, :]).astyp...  8.79 us
  transfers between devices with their start and end apart: 1, of which 0 were waited for; matrix products, arithmetic and copies ran while one was open for 14% of the time, Pallas kernels for 0%

profile of v5, /device:TPU:0, one launch (start us, length us, event | category | flops | bytes accessed | tf_op | source)
XLA Modules:
  0.0 276.1 jit_solution(1028274802466911577)
XLA Ops:
  0.0 0.8 fusion.56
  2.3 0.8 fusion.55
  4.0 1.4 fusion.31
  5.8 0.8 pad_maximum_fusion.1
  6.6 7.3 %all-to-all-start = ((f32[8,97,128]{2,1,0:T(8,128)}), f32[8,97,128]{2,1,0:T(8,128)}, u32[]{:S(2)}, u32[]{:S(2)}) async-start(f32[8,97,128]{2,1,0:T(8,128)} %pad_maximum_fusion.1), calls=%async_computation | async-start | bytes 851968 | tf_op jit(solution)/shard_map/all_to_all | solution.py:122
  13.9 1.4 slice_bitcast_fusion.1
  15.3 1.0 fusion.72
  16.5 1.1 fusion.39
  18.0 2.0 subtract_convert_fusion.2
  20.7 2.1 copy.47
  22.7 3.1 %reshape.801.u_ref = bf16[32,64,128]{2,1,0:T(8,128)(2,1)} reshape(bf16[32,64,2,64]{3,2,1,0:T(2,128)(2,1)} %copy.47) | data formatting | bytes 1048576 | tf_op jit(solution)/shard_map/reshape | solution.py:63
  25.8 4.5 %convert_element_type.165 = bf16[4,256,1,1024]{1,0,3,2:T(4,128)(2,1)} reshape(bf16[1024,16,64]{0,2,1:T(8,128)(2,1)} %subtract_convert_fusion.2) | data formatting | bytes 4194304 | tf_op jit(solution)/shard_map/convert_element_type | solution.py:179
  30.3 4.3 %copy.39 = bf16[4,256,1,1024]{3,1,2,0:T(8,128)(2,1)} copy(bf16[4,256,1,1024]{1,0,3,2:T(4,128)(2,1)} %convert_element_type.165) | data formatting | bytes 4194304 | tf_op jit(solution)/shard_map/convert_element_type | solution.py:179
  34.6 2.7 neg.21
  37.3 4.4 %copy.40 = bf16[4,256,1,1024]{3,1,2,0:T(8,128)(2,1)} copy(bf16[4,256,1,1024]{1,0,3,2:T(4,128)(2,1)} %neg.21) | data formatting | bytes 4194304 | tf_op jit(solution)/shard_map/neg | solution.py:183
  42.4 1.1 pad_maximum_fusion.v_ref
  44.2 1.3 fusion.44
  45.5 5.9 %fusion.27 = (f32[8,128,256]{2,1,0:T(8,128)}, f32[8,128,256]{2,1,0:T(8,128)}) fusion(s32[8,256]{1,0:T(8,128)S(1)} %add_multiply_fusion, s32[128]{0:T(128)S(1)} %and_select_fusion), kind=kLoop, calls=%fused_computation.46 | loop fusion | flops 3670016 | bytes 2105856 | tf_op jit(solution)/shard_map/cos | solution.py:96
  51.5 0.8 fusion.59
  53.1 1.0 slice.40
  54.1 0.9 copy.45
  55.0 20.0 %shard_map.55 = bf16[768,2,64,128]{3,2,1,0:T(8,128)(2,1)} custom-call(s32[768]{0:T(1024)} %get-tuple-element.20.plane_ref, f32[128,768]{1,0:T(8,128)} %bitcast.100, bf16[32,64,128]{2,1,0:T(8,128)(2,1)} %reshape.801.u_ref, bf16[32,2,64,128]{3,2,1,0:T(8,128)(2,1)} %pad_maximum_fusion.v_ref), custom_call_target="tpu_custom_call" | custom-call | flops 3221225472 | bytes 50331648 | tf_op jit(solution)/shard_map/pallas_call | solution.py:79
  75.0 34.8 %reshape.802 = bf16[768,2,8192]{2,1,0:T(2,128)(2,1)} reshape(bf16[768,2,64,128]{3,2,1,0:T(8,128)(2,1)} %shard_map.55) | data formatting | bytes 50331648 | tf_op jit(solution)/shard_map/reshape | solution.py:138
  109.9 1.9 multiply_convert_fusion.4
  111.9 60.7 %bitcast_convert_fusion = bf16[8,16,16,8192]{3,2,1,0:T(8,128)(2,1)} fusion(bf16[768,2,8192,1,1]{2,1,0,4,3:T(2,128)(2,1)} %bitcast.93, bf16[8,16,16,768,2]{3,2,4,1,0:T(8,128)(2,1)S(1)} %multiply_convert_fusion.4), kind=kOutput, calls=%fused_computation | convolution fusion | flops 51556384768 | bytes 65011712 | tf_op jit(solution)/shard_map/raqsk,skn->raqn/dot_general | solution.py:153
  172.6 23.2 %copy.65 = bf16[256,8,64,128]{3,2,1,0:T(8,128)(2,1)} copy(bf16[256,8,64,128]{3,1,2,0:T(8,128)(2,1)} %bitcast.92) | data formatting | bytes 67108864
  195.8 16.2 %bitcast_convert_fusion.1 = bf16[8,16,64,256]{3,2,1,0:T(8,128)(2,1)} fusion(bf16[8,16,16,64,128]{4,3,2,1,0:T(8,128)(2,1)} %bitcast.91, f32[8,128,256]{2,1,0:T(8,128)S(1)} %copy-done.5, f32[8,16,256]{2,1,0:T(8,128)S(1)} %copy-done.8, f32[8,128,256]{2,1,0:T(8,128)S(1)} %copy-done.4, f32[8,16,256]{2,1,0:T(8,128)S(1)} %copy-done.7, ...), kind=kOutput, calls=%fused_computation.9 | convolution fusion | flops 8638169088 | bytes 40173568 | tf_op jit(solution)/shard_map/raqxk,rqkn->raxn/dot_general | solution.py:172
  212.0 7.1 %reshape.804 = bf16[8,1024,2,128]{3,2,1,0:T(2,128)(2,1)} reshape(bf16[8,16,64,256]{3,2,1,0:T(8,128)(2,1)} %bitcast_convert_fusion.1) | data formatting | bytes 8388608 | tf_op jit(solution)/shard_map/reshape | solution.py:173
  219.0 7.3 %bitcast_convert_fusion.2 = bf16[4,256,8,128]{3,1,2,0:T(8,128)(2,1)S(1)} fusion(bf16[8,1024,2,128]{3,2,1,0:T(2,128)(2,1)} %reshape.804, bf16[4,256,1,1024]{3,1,2,0:T(8,128)(2,1)} %copy.40, bf16[4,256,1,1024]{3,1,2,0:T(8,128)(2,1)S(1)} %copy-done.1), kind=kOutput, calls=%fused_computation.22 | convolution fusion | flops 4304404480 | bytes 10485760 | tf_op jit(solution)/shard_map/liu,ruij->lrj/dot_general | solution.py:184
  226.3 28.3 %all_to_all.15 = bf16[4,256,8,128]{3,1,2,0:T(8,128)(2,1)S(1)} all-to-all(bf16[4,256,8,128]{3,1,2,0:T(8,128)(2,1)S(1)} %bitcast_convert_fusion.2), channel_id=1, replica_groups=mesh['tile'=8,'chan'=4] {'chan'}, dimensions={0} | all-to-all | bytes 4194304 | tf_op jit(solution)/shard_map/all_to_all | solution.py:187
  255.3 19.9 %all_to_all.16 = bf16[8,256,8,16]{1,3,2,0:T(8,128)(2,1)S(1)} all-to-all(bf16[8,256,8,16]{1,3,2,0:T(8,128)(2,1)S(1)} %copy.52), channel_id=1, replica_groups=mesh['tile'=8,'chan'=4] {'tile'}, dimensions={0} | all-to-all | bytes 1048576 | tf_op jit(solution)/shard_map/all_to_all | solution.py:191
  275.4 0.8 copy.55
  (68 shorter events, 7.0 us)
Async XLA Ops:
  0.0 13.9 %copy-start.6 = (bf16[1,32,2,64,128]{4,3,2,1,0:T(8,128)(2,1)S(1)}, bf16[1,32,2,64,128]{4,3,2,1,0:T(8,128)(2,1)}, u32[]{:S(2)}) copy-start(bf16[1,32,2,64,128]{4,3,2,1,0:T(8,128)(2,1)} %param.6) | copy-start | bytes 3145732
  6.6 44.8 %all-to-all-start = ((f32[8,97,128]{2,1,0:T(8,128)}), f32[8,97,128]{2,1,0:T(8,128)}, u32[]{:S(2)}, u32[]{:S(2)}) async-start(f32[8,97,128]{2,1,0:T(8,128)} %pad_maximum_fusion.1), calls=%async_computation | async-start | bytes 851968 | tf_op jit(solution)/shard_map/all_to_all | solution.py:122
  34.6 7.2 %copy-start = (bf16[32,64,64]{2,1,0:T(8,128)(2,1)S(1)}, bf16[32,64,64]{2,1,0:T(8,128)(2,1)}, u32[]{:S(2)}) copy-start(bf16[32,64,64]{2,1,0:T(8,128)(2,1)} %fusion.72) | copy-start | bytes 786436
  34.6 7.2 %copy-start.2 = (bf16[32,64,64]{2,1,0:T(8,128)(2,1)S(1)}, bf16[32,64,64]{2,1,0:T(8,128)(2,1)}, u32[]{:S(2)}) copy-start(bf16[32,64,64]{2,1,0:T(8,128)(2,1)} %get-tuple-element.5) | copy-start | bytes 786436
  37.3 4.4 %copy-start.3 = (bf16[32,64,64]{2,1,0:T(8,128)(2,1)S(1)}, bf16[32,64,64]{2,1,0:T(8,128)(2,1)}, u32[]{:S(2)}) copy-start(bf16[32,64,64]{2,1,0:T(8,128)(2,1)} %get-tuple-element.6) | copy-start | bytes 786436
  172.5 23.2 %copy-start.4 = (f32[8,128,256]{2,1,0:T(8,128)S(1)}, f32[8,128,256]{2,1,0:T(8,128)}, u32[]{:S(2)}) copy-start(f32[8,128,256]{2,1,0:T(8,128)} %get-tuple-element.11) | copy-start | bytes 3145732
  172.5 23.2 %copy-start.5 = (f32[8,128,256]{2,1,0:T(8,128)S(1)}, f32[8,128,256]{2,1,0:T(8,128)}, u32[]{:S(2)}) copy-start(f32[8,128,256]{2,1,0:T(8,128)} %get-tuple-element.12) | copy-start | bytes 3145732
  172.5 23.2 %copy-start.7 = (f32[8,16,256]{2,1,0:T(8,128)S(1)}, f32[8,16,256]{2,1,0:T(8,128)}, u32[]{:S(2)}) copy-start(f32[8,16,256]{2,1,0:T(8,128)} %get-tuple-element.9) | copy-start | bytes 393220
  172.5 23.2 %copy-start.8 = (f32[8,16,256]{2,1,0:T(8,128)S(1)}, f32[8,16,256]{2,1,0:T(8,128)}, u32[]{:S(2)}) copy-start(f32[8,16,256]{2,1,0:T(8,128)} %get-tuple-element.10) | copy-start | bytes 393220
  172.5 23.2 %copy-start.9 = (pred[128,256]{1,0:T(8,128)(4,1)S(1)}, pred[128,256]{1,0:T(8,128)(4,1)}, u32[]{:S(2)}) copy-start(pred[128,256]{1,0:T(8,128)(4,1)} %get-tuple-element.23) | copy-start | bytes 98308
  172.6 23.2 %copy-start.10 = (pred[128,256]{1,0:T(8,128)(4,1)S(1)}, pred[128,256]{1,0:T(8,128)(4,1)}, u32[]{:S(2)}) copy-start(pred[128,256]{1,0:T(8,128)(4,1)} %get-tuple-element.24) | copy-start | bytes 98308
  212.0 7.1 %copy-start.1 = (bf16[4,256,1,1024]{3,1,2,0:T(8,128)(2,1)S(1)}, bf16[4,256,1,1024]{3,1,2,0:T(8,128)(2,1)}, u32[]{:S(2)}) copy-start(bf16[4,256,1,1024]{3,1,2,0:T(8,128)(2,1)} %copy.39) | copy-start | bytes 6291460

commit v6 on v5

--- a/solution.py
+++ b/solution.py
@@ -135,7 +135,7 @@
 
     cell_r = arrived_meta // NW
     plane_r = arrived_meta % NW
-    p2 = patches_rotated(arrived, plane_r, kernel_set).reshape(slot_total, 2, S * 2 * S)
+    p2 = patches_rotated(arrived, plane_r, kernel_set).reshape(slot_total * 2, S * 2 * S)
 
     a_s = cell_r // cell_cols
     cc_s = cell_r % cell_cols
@@ -150,7 +150,8 @@
     )[:, None, :]
     l2 = (place.astype(jnp.float32)[None, :, :, :, None] * jnp.transpose(phase, (1, 0, 2))[:, :, None, None, :])
     l2 = jnp.transpose(l2, (0, 2, 3, 1, 4)).astype(jnp.bfloat16)
-    folded = jnp.einsum("raqsk,skn->raqn", l2, p2, preferred_element_type=jnp.float32).astype(jnp.bfloat16)
+    l2 = l2.reshape(NF * row_cells * q_cells, slot_total * 2)
+    folded = jnp.dot(l2, p2, preferred_element_type=jnp.float32).astype(jnp.bfloat16)
     folded = folded.reshape(NF, row_cells, q_cells, S, 2 * S)
 
     coarse = jnp.arange(q_cells, dtype=jnp.int32) * S

time: 278 us -> 345 us (1.24)
  local copies, waits for them, and re-layouts: 91.4 us -> 143 us
  other arithmetic: 23.3 us -> 40.2 us
    convert_element_type x0 -> x1, local copies, waits for them, and re-layouts: none -> 85.5 us  [local(): l2 = jnp.transpose(l2, (0, 2, 3, 1, 4)).astype(jnp.bfloat16)]
    reshape x1 -> x0, local copies, waits for them, and re-layouts: 34.8 us -> none  [local(): patches_rotated(arrived, plane_r, kernel_set)]
    convert_element_type x0 -> x1, other arithmetic: none -> 16.7 us  [local(): l2 = jnp.transpose(l2, (0, 2, 3, 1, 4)).astype(jnp.bfloat16)]
  transfers between devices with their start and end apart: 1 -> 1, of which waited for: 0 -> 0; matrix products, arithmetic and copies ran while one was open for 14% -> 11% of each run, Pallas kernels for 0% -> 0%
where the time goes in v6:
time: 345 us; the launch traced here: 344 us
  local copies, waits for them, and re-layouts  143 us (41%)
  matrix products  85.4 us (25%)
  blocking collectives  48.2 us (14%)
  other arithmetic  40.2 us (12%)
  Pallas kernels  20 us (6%)
  starting transfers between devices  7.25 us (2%)
    convert_element_type x1, local copies, waits for them, and re-layouts, local(): l2 = jnp.transpose(l2, (0, 2, 3, 1, 4)).astype(jnp.bfloat16)  85.5 us
    dot_general x1, matrix products, local(): jnp.dot(l2, p2, preferred_element_type=jnp.float32).astype(jnp.bfloat16)  60.5 us
    all_to_all x1, blocking collectives, local(): lax.all_to_all(partial.astype(jnp.bfloat16), 'chan', split_axis=0, concat...  28.3 us
    unnamed x24, local copies, waits for them, and re-layouts  23.3 us
    pallas_call x1, Pallas kernels, patches_rotated(): pl.pallas_call(patch_kernel, grid_spec=grid_spec, out_shape=jax.ShapeDtyp...  20 us
    all_to_all x1, blocking collectives, local(): lax.all_to_all(partial.astype(jnp.bfloat16), 'tile', split_axis=0, concat...  19.9 us
    convert_element_type x1, other arithmetic, local(): l2 = jnp.transpose(l2, (0, 2, 3, 1, 4)).astype(jnp.bfloat16)  16.7 us
    dot_general x1, matrix products, local(): jnp.einsum('raqxk,rqkn->raxn', folded, w1, preferred_element_type=jnp.flo...  16.1 us
  transfers between devices with their start and end apart: 1, of which 0 were waited for; matrix products, arithmetic and copies ran while one was open for 11% of the time, Pallas kernels for 0%

profile of v6, /device:TPU:0, one launch (start us, length us, event | category | flops | bytes accessed | tf_op | source)
XLA Modules:
  0.0 344.0 jit_solution(13897983708002210356)
XLA Ops:
  0.0 0.8 fusion.55
  2.3 0.8 fusion.54
  4.0 1.4 fusion.30
  5.8 0.8 pad_maximum_fusion.1
  6.6 7.3 %all-to-all-start = ((f32[8,97,128]{2,1,0:T(8,128)}), f32[8,97,128]{2,1,0:T(8,128)}, u32[]{:S(2)}, u32[]{:S(2)}) async-start(f32[8,97,128]{2,1,0:T(8,128)} %pad_maximum_fusion.1), calls=%async_computation | async-start | bytes 851968 | tf_op jit(solution)/shard_map/all_to_all | solution.py:122
  13.9 1.4 slice_bitcast_fusion.1
  15.3 1.0 fusion.71
  16.5 1.1 fusion.38
  18.0 2.0 subtract_convert_fusion.2
  20.7 2.1 copy.29
  22.7 3.1 reshape.814.u_ref
  25.8 4.5 %convert_element_type.175 = bf16[4,256,1,1024]{1,0,3,2:T(4,128)(2,1)} reshape(bf16[1024,16,64]{0,2,1:T(8,128)(2,1)} %subtract_convert_fusion.2) | data formatting | bytes 4194304 | tf_op jit(solution)/shard_map/convert_element_type | solution.py:180
  30.3 4.3 %copy.21 = bf16[4,256,1,1024]{3,1,2,0:T(8,128)(2,1)} copy(bf16[4,256,1,1024]{1,0,3,2:T(4,128)(2,1)} %convert_element_type.175) | data formatting | bytes 4194304 | tf_op jit(solution)/shard_map/convert_element_type | solution.py:180
  34.6 2.8 neg.21
  37.4 4.4 %copy.22 = bf16[4,256,1,1024]{3,1,2,0:T(8,128)(2,1)} copy(bf16[4,256,1,1024]{1,0,3,2:T(4,128)(2,1)} %neg.21) | data formatting | bytes 4194304 | tf_op jit(solution)/shard_map/neg | solution.py:184
  42.4 1.2 pad_maximum_fusion.v_ref
  44.3 1.3 fusion.43
  45.6 5.9 %fusion.26 = (f32[8,128,256]{2,1,0:T(8,128)}, f32[8,128,256]{2,1,0:T(8,128)}) fusion(s32[8,256]{1,0:T(8,128)S(1)} %add_multiply_fusion, s32[128]{0:T(128)S(1)} %and_select_fusion), kind=kLoop, calls=%fused_computation.45 | loop fusion | flops 3670016 | bytes 2105856 | tf_op jit(solution)/shard_map/cos | solution.py:96
  51.6 0.8 fusion.58
  53.9 2.0 and_convert_fusion
  55.8 16.7 %multiply_convert_fusion = bf16[8,16,16,768,2]{2,1,0,4,3:T(8,128)(2,1)} fusion(f32[8,768,2]{0,2,1:T(2,128)S(1)} %copy.26, f32[16,16,768]{1,0,2:T(8,128)S(1)} %and_convert_fusion), kind=kLoop, calls=%fused_computation | loop fusion | flops 6291456 | bytes 7127040 | tf_op jit(solution)/shard_map/convert_element_type | solution.py:152
  72.5 85.5 %convert_element_type.185 = bf16[2048,1536]{0,1:T(8,128)(2,1)} reshape(bf16[8,16,16,768,2]{2,1,0,4,3:T(8,128)(2,1)} %multiply_convert_fusion) | data formatting | bytes 12582912 | tf_op jit(solution)/shard_map/convert_element_type | solution.py:152
  158.0 1.0 slice.40
  159.0 0.9 copy.27
  159.9 20.0 %shard_map.55 = bf16[768,2,64,128]{3,2,1,0:T(8,128)(2,1)} custom-call(s32[768]{0:T(1024)} %get-tuple-element.17.plane_ref, f32[128,768]{1,0:T(8,128)} %bitcast.100, bf16[32,64,128]{2,1,0:T(8,128)(2,1)} %reshape.814.u_ref, bf16[32,2,64,128]{3,2,1,0:T(8,128)(2,1)} %pad_maximum_fusion.v_ref), custom_call_target="tpu_custom_call" | custom-call | flops 3221225472 | bytes 50331648 | tf_op jit(solution)/shard_map/pallas_call | solution.py:79
  179.9 60.5 %convert_bitcast_fusion = bf16[256,8,64,128]{3,1,2,0:T(8,128)(2,1)} fusion(bf16[2048,1536]{0,1:T(8,128)(2,1)} %convert_element_type.185, bf16[192,8,64,128]{3,2,1,0:T(8,128)(2,1)} %bitcast.93), kind=kOutput, calls=%fused_computation.1 | convolution fusion | flops 51556384768 | bytes 65011712 | tf_op jit(solution)/shard_map/dot_general | solution.py:154
  240.5 23.1 %copy.43 = bf16[256,8,64,128]{3,2,1,0:T(8,128)(2,1)} copy(bf16[256,8,64,128]{3,1,2,0:T(8,128)(2,1)} %convert_bitcast_fusion) | data formatting | bytes 67108864
  263.7 16.1 %bitcast_convert_fusion = bf16[8,16,64,256]{3,2,1,0:T(8,128)(2,1)} fusion(bf16[8,16,16,64,128]{4,3,2,1,0:T(8,128)(2,1)} %bitcast.92, f32[8,128,256]{2,1,0:T(8,128)S(1)} %copy-done.5, f32[8,16,256]{2,1,0:T(8,128)S(1)} %copy-done.8, f32[8,128,256]{2,1,0:T(8,128)S(1)} %copy-done.4, f32[8,16,256]{2,1,0:T(8,128)S(1)} %copy-done.7, ...), kind=kOutput, calls=%fused_computation.10 | convolution fusion | flops 8638169088 | bytes 40173568 | tf_op jit(solution)/shard_map/raqxk,rqkn->raxn/dot_general | solution.py:173
  279.8 7.1 %reshape.817 = bf16[8,1024,2,128]{3,2,1,0:T(2,128)(2,1)} reshape(bf16[8,16,64,256]{3,2,1,0:T(8,128)(2,1)} %bitcast_convert_fusion) | data formatting | bytes 8388608 | tf_op jit(solution)/shard_map/reshape | solution.py:174
  286.9 7.3 %bitcast_convert_fusion.1 = bf16[4,256,8,128]{3,1,2,0:T(8,128)(2,1)S(1)} fusion(bf16[8,1024,2,128]{3,2,1,0:T(2,128)(2,1)} %reshape.817, bf16[4,256,1,1024]{3,1,2,0:T(8,128)(2,1)} %copy.22, bf16[4,256,1,1024]{3,1,2,0:T(8,128)(2,1)S(1)} %copy-done.1), kind=kOutput, calls=%fused_computation.22 | convolution fusion | flops 4304404480 | bytes 10485760 | tf_op jit(solution)/shard_map/liu,ruij->lrj/dot_general | solution.py:185
  294.2 28.3 %all_to_all.15 = bf16[4,256,8,128]{3,1,2,0:T(8,128)(2,1)S(1)} all-to-all(bf16[4,256,8,128]{3,1,2,0:T(8,128)(2,1)S(1)} %bitcast_convert_fusion.1), channel_id=1, replica_groups=mesh['tile'=8,'chan'=4] {'chan'}, dimensions={0} | all-to-all | bytes 4194304 | tf_op jit(solution)/shard_map/all_to_all | solution.py:188
  323.2 19.9 %all_to_all.16 = bf16[8,256,8,16]{1,3,2,0:T(8,128)(2,1)S(1)} all-to-all(bf16[8,256,8,16]{1,3,2,0:T(8,128)(2,1)S(1)} %copy.33), channel_id=1, replica_groups=mesh['tile'=8,'chan'=4] {'tile'}, dimensions={0} | all-to-all | bytes 1048576 | tf_op jit(solution)/shard_map/all_to_all | solution.py:192
  (68 shorter events, 8.4 us)
Async XLA Ops:
  0.0 13.8 %copy-start.6 = (bf16[1,32,2,64,128]{4,3,2,1,0:T(8,128)(2,1)S(1)}, bf16[1,32,2,64,128]{4,3,2,1,0:T(8,128)(2,1)}, u32[]{:S(2)}) copy-start(bf16[1,32,2,64,128]{4,3,2,1,0:T(8,128)(2,1)} %param.6) | copy-start | bytes 3145732
  6.6 45.0 %all-to-all-start = ((f32[8,97,128]{2,1,0:T(8,128)}), f32[8,97,128]{2,1,0:T(8,128)}, u32[]{:S(2)}, u32[]{:S(2)}) async-start(f32[8,97,128]{2,1,0:T(8,128)} %pad_maximum_fusion.1), calls=%async_computation | async-start | bytes 851968 | tf_op jit(solution)/shard_map/all_to_all | solution.py:122
  34.6 7.2 %copy-start = (bf16[32,64,64]{2,1,0:T(8,128)(2,1)S(1)}, bf16[32,64,64]{2,1,0:T(8,128)(2,1)}, u32[]{:S(2)}) copy-start(bf16[32,64,64]{2,1,0:T(8,128)(2,1)} %fusion.71) | copy-start | bytes 786436
  34.6 7.2 %copy-start.2 = (bf16[32,64,64]{2,1,0:T(8,128)(2,1)S(1)}, bf16[32,64,64]{2,1,0:T(8,128)(2,1)}, u32[]{:S(2)}) copy-start(bf16[32,64,64]{2,1,0:T(8,128)(2,1)} %get-tuple-element.5) | copy-start | bytes 786436
  37.4 4.4 %copy-start.3 = (bf16[32,64,64]{2,1,0:T(8,128)(2,1)S(1)}, bf16[32,64,64]{2,1,0:T(8,128)(2,1)}, u32[]{:S(2)}) copy-start(bf16[32,64,64]{2,1,0:T(8,128)(2,1)} %get-tuple-element.6) | copy-start | bytes 786436
  240.5 23.2 %copy-start.4 = (f32[8,128,256]{2,1,0:T(8,128)S(1)}, f32[8,128,256]{2,1,0:T(8,128)}, u32[]{:S(2)}) copy-start(f32[8,128,256]{2,1,0:T(8,128)} %get-tuple-element.11) | copy-start | bytes 3145732
  240.5 23.2 %copy-start.5 = (f32[8,128,256]{2,1,0:T(8,128)S(1)}, f32[8,128,256]{2,1,0:T(8,128)}, u32[]{:S(2)}) copy-start(f32[8,128,256]{2,1,0:T(8,128)} %get-tuple-element.12) | copy-start | bytes 3145732
  240.5 23.2 %copy-start.7 = (f32[8,16,256]{2,1,0:T(8,128)S(1)}, f32[8,16,256]{2,1,0:T(8,128)}, u32[]{:S(2)}) copy-start(f32[8,16,256]{2,1,0:T(8,128)} %get-tuple-element.9) | copy-start | bytes 393220
  240.5 23.2 %copy-start.8 = (f32[8,16,256]{2,1,0:T(8,128)S(1)}, f32[8,16,256]{2,1,0:T(8,128)}, u32[]{:S(2)}) copy-start(f32[8,16,256]{2,1,0:T(8,128)} %get-tuple-element.10) | copy-start | bytes 393220
  240.5 23.2 %copy-start.9 = (pred[128,256]{1,0:T(8,128)(4,1)S(1)}, pred[128,256]{1,0:T(8,128)(4,1)}, u32[]{:S(2)}) copy-start(pred[128,256]{1,0:T(8,128)(4,1)} %get-tuple-element.23) | copy-start | bytes 98308
  240.5 23.2 %copy-start.10 = (pred[128,256]{1,0:T(8,128)(4,1)S(1)}, pred[128,256]{1,0:T(8,128)(4,1)}, u32[]{:S(2)}) copy-start(pred[128,256]{1,0:T(8,128)(4,1)} %get-tuple-element.24) | copy-start | bytes 98308
  279.8 7.1 %copy-start.1 = (bf16[4,256,1,1024]{3,1,2,0:T(8,128)(2,1)S(1)}, bf16[4,256,1,1024]{3,1,2,0:T(8,128)(2,1)}, u32[]{:S(2)}) copy-start(bf16[4,256,1,1024]{3,1,2,0:T(8,128)(2,1)} %copy.21) | copy-start | bytes 6291460
